TPU v7x, 128 devices: a whole 4x4x4 slice. The times are simulated.
128 devices in a mesh: kz: 4 (over x_hi, core), en: 32 (over z, y, x_lo).
Axes of the slice: x: 4 (x_hi: 2, x_lo: 2; x = x_hi * 2 + x_lo), y: 4, z: 4, core: 2. Of those that a mesh axis runs over, the one named last changes fastest.
Arguments:
- sigma_less: bfloat16 [4, 128, 3, 2, 128, 128], P('kz', 'en'), as said below
- sigma_great: bfloat16 [4, 128, 3, 2, 128, 128], P('kz', 'en'), as said below
- onsite_table: float32 [3, 128, 128], replicated, as said below
- cos_coupling: float32 [3, 128, 128], replicated, as said below
- slab_coupling: float32 [2, 128, 128], replicated, may hold values from -0.25 to 0.25
- slab_kind: int32 [3], replicated, may hold values from 0 to 2, as said below
- kz_table: int32 [4, 4], replicated, may hold values from 0 to 3, as said below
- mode_weight: float32 [2, 4], replicated, may hold values from 0.25 to 2
- form_factor: float32 [2, 128, 128], replicated, as said below
- occupation: float32 [2], replicated, may hold values from 0.1 to 2
- energy_offset: int32 [2], replicated, may hold values from 1 to 4, as said below
Outputs:
- sigma_less_new: bfloat16 [4, 128, 3, 2, 128, 128], P('kz', 'en')
- sigma_great_new: bfloat16 [4, 128, 3, 2, 128, 128], P('kz', 'en')
Inputs may be any that keep to these rules, and one draw needn't show every extreme that they name: `sigma_less`: each block is i times a Hermitian matrix. `sigma_great`: each block is -i times a Hermitian matrix. `onsite_table`: each block is symmetric. `cos_coupling`: each block is symmetric. `form_factor`: each block is symmetric and positive. `kz_table`: each row names every momentum once. `slab_kind`: every kind is used by some slab. `energy_offset`: the modes have different offsets, and some mode has exactly 4.
All inputs are finite; a program needn't handle non-finite values.
Results may differ from a plain program's by a relative error of at most 0.0029.
Values may be sent and summed in bfloat16 or wider, within the bound.
No kernel may reach another device: no remote copies, remote signals or barrier semaphores. Data moves between devices by JAX's collectives and lax.ppermute only.
A program may use at most 128 MiB of HBM per device.

v0:
```python
import jax
import jax.numpy as jnp
from jax import lax
from jax.sharding import PartitionSpec as P

OFFMAX = 4


DAMPING = 0.3


def padded(block, sides, width):
    for axis, dim in sides:
        count = lax.axis_size(axis)
        forward = [(i, i + 1) for i in range(count - 1)]
        backward = [(target, source) for source, target in forward]
        low = lax.ppermute(
            lax.slice_in_dim(block, block.shape[dim] - width, None, axis=dim), axis, forward
        )
        high = lax.ppermute(lax.slice_in_dim(block, 0, width, axis=dim), axis, backward)
        block = jnp.concatenate([low, block, high], axis=dim)
    return block


def matmul_high(left_matrix, right_matrix):
    return jnp.matmul(left_matrix, right_matrix, precision=lax.Precision.HIGHEST)


def complex_product(left_pair, right_pair):
    real_part = matmul_high(left_pair[0], right_pair[0]) - matmul_high(left_pair[1], right_pair[1])
    imag_part = matmul_high(left_pair[0], right_pair[1]) + matmul_high(left_pair[1], right_pair[0])
    return (real_part, imag_part)


def real_left(matrix, pair_value):
    return (matmul_high(matrix, pair_value[0]), matmul_high(matrix, pair_value[1]))


def real_right(pair_value, matrix):
    return (matmul_high(pair_value[0], matrix), matmul_high(pair_value[1], matrix))


def adjoint(pair_value):
    return (jnp.swapaxes(pair_value[0], -1, -2), -jnp.swapaxes(pair_value[1], -1, -2))


def add_pair(left_pair, right_pair):
    return (left_pair[0] + right_pair[0], left_pair[1] + right_pair[1])


def sub_pair(left_pair, right_pair):
    return (left_pair[0] - right_pair[0], left_pair[1] - right_pair[1])


def invert_pair(pair_value):
    orbitals = pair_value[0].shape[-1]
    upper_half = jnp.concatenate([pair_value[0], -pair_value[1]], axis=-1)
    lower_half = jnp.concatenate([pair_value[1], pair_value[0]], axis=-1)
    embedded = jnp.concatenate([upper_half, lower_half], axis=-2)
    transposed = jnp.swapaxes(embedded, -1, -2)
    normal = matmul_high(transposed, embedded)
    factor = jnp.linalg.cholesky(normal)
    solved = jax.scipy.linalg.cho_solve((factor, True), transposed)
    return (solved[..., :orbitals, :orbitals], solved[..., orbitals:, :orbitals])


def greater_of(less_pair, ret_pair):
    return sub_pair(add_pair(less_pair, ret_pair), adjoint(ret_pair))


def pack_pair(pair_value):
    return jnp.stack([pair_value[0], pair_value[1]], axis=-3)


def green_blocks(sigma_less, sigma_great, hamilton, slab_coupling, energies):
    orbitals = sigma_less.shape[-1]
    slab_count = sigma_less.shape[2]
    identity = jnp.eye(orbitals, dtype=jnp.float32)
    energy_grid = energies[None, :, None, None]
    left_ret = []
    left_less = []
    for slab_index in range(slab_count):
        lesser = sigma_less[:, :, slab_index].astype(jnp.float32)
        greater = sigma_great[:, :, slab_index].astype(jnp.float32)
        retarded_re = 0.5 * (greater[:, :, 0] - lesser[:, :, 0])
        retarded_im = 0.5 * (greater[:, :, 1] - lesser[:, :, 1]) - DAMPING * identity
        system_re = energy_grid * identity - hamilton[:, :, slab_index] - retarded_re
        system_im = -retarded_im
        source = (lesser[:, :, 0], lesser[:, :, 1])
        if slab_index > 0:
            coupling = slab_coupling[slab_index - 1]
            folded = real_right(real_left(coupling, left_ret[-1]), coupling.T)
            system_re = system_re - folded[0]
            system_im = system_im - folded[1]
            source = add_pair(source, real_right(real_left(coupling, left_less[-1]), coupling.T))
        inverse = invert_pair((system_re, system_im))
        left_ret.append(inverse)
        left_less.append(complex_product(complex_product(inverse, source), adjoint(inverse)))
    full_ret = left_ret[-1]
    full_less = left_less[-1]
    lesser_list = [full_less]
    greater_list = [greater_of(full_less, full_ret)]
    for slab_index in range(slab_count - 2, -1, -1):
        coupling = slab_coupling[slab_index]
        green_couple = real_right(left_ret[slab_index], coupling)
        bridge = real_right(complex_product(green_couple, full_ret), coupling.T)
        cross_term = complex_product(bridge, left_less[slab_index])
        spread = complex_product(
            real_right(complex_product(green_couple, full_less), coupling.T),
            adjoint(left_ret[slab_index]),
        )
        full_less = add_pair(
            add_pair(left_less[slab_index], spread), sub_pair(cross_term, adjoint(cross_term))
        )
        full_ret = add_pair(left_ret[slab_index], complex_product(bridge, left_ret[slab_index]))
        lesser_list.insert(0, full_less)
        greater_list.insert(0, greater_of(full_less, full_ret))
    lesser_all = jnp.stack([pack_pair(item) for item in lesser_list], axis=2)
    greater_all = jnp.stack([pack_pair(item) for item in greater_list], axis=2)
    return jnp.stack([lesser_all, greater_all], axis=2).astype(jnp.bfloat16)


def hamiltonian(onsite_table, cos_coupling, slab_kind, momenta_index, momenta_total):
    kind_count = onsite_table.shape[0]
    choose = (slab_kind[:, None] == jnp.arange(kind_count, dtype=jnp.int32)[None, :]).astype(
        jnp.float32
    )
    onsite = jnp.einsum("sk,kij->sij", choose, onsite_table, precision=lax.Precision.HIGHEST)
    phase_factor = jnp.cos(2.0 * jnp.pi * momenta_index.astype(jnp.float32) / momenta_total)
    hamilton = onsite[None] + phase_factor[:, None, None, None] * cos_coupling[None]
    return hamilton[:, None]


def momentum_weights(table_rows, mode_weight, momenta_total):
    onehot = (
        table_rows[:, :, None] == jnp.arange(momenta_total, dtype=jnp.int32)[None, None, :]
    ).astype(jnp.float32)
    return (
        jnp.einsum("lq,aqk->lak", mode_weight, onehot, precision=lax.Precision.HIGHEST)
        / momenta_total
    )


def mixed_sums(extended, weights, form_factor, occupation, energy_offset, energy_count, margin):
    total_less = None
    total_great = None
    for mode_index in range(form_factor.shape[0]):
        shift_steps = energy_offset[mode_index]
        upper_side = lax.dynamic_slice_in_dim(extended, margin + shift_steps, energy_count, 1)
        lower_side = lax.dynamic_slice_in_dim(extended, margin - shift_steps, energy_count, 1)
        occupied = occupation[mode_index]
        less_term = (occupied + 1.0) * upper_side[:, :, 0].astype(
            jnp.float32
        ) + occupied * lower_side[:, :, 0].astype(jnp.float32)
        great_term = (occupied + 1.0) * lower_side[:, :, 1].astype(
            jnp.float32
        ) + occupied * upper_side[:, :, 1].astype(jnp.float32)
        less_sum = form_factor[mode_index] * jnp.einsum(
            "ak,kesrij->aesrij", weights[mode_index], less_term, precision=lax.Precision.HIGHEST
        )
        great_sum = form_factor[mode_index] * jnp.einsum(
            "ak,kesrij->aesrij", weights[mode_index], great_term, precision=lax.Precision.HIGHEST
        )
        total_less = less_sum if total_less is None else total_less + less_sum
        total_great = great_sum if total_great is None else total_great + great_sum
    return (total_less, total_great)


def on_device(
    sigma_less,
    sigma_great,
    onsite_table,
    cos_coupling,
    slab_coupling,
    slab_kind,
    kz_table,
    mode_weight,
    form_factor,
    occupation,
    energy_offset,
):
    momenta_local = sigma_less.shape[0]
    energy_local = sigma_less.shape[1]
    momenta_total = momenta_local * lax.axis_size("kz")
    energy_total = energy_local * lax.axis_size("en")
    momenta_start = lax.axis_index("kz") * momenta_local
    momenta_index = momenta_start + jnp.arange(momenta_local, dtype=jnp.int32)
    energy_index = lax.axis_index("en") * energy_local + jnp.arange(energy_local, dtype=jnp.int32)
    energies = -1.5 + 3.0 * (energy_index.astype(jnp.float32) + 0.5) / energy_total
    hamilton = hamiltonian(onsite_table, cos_coupling, slab_kind, momenta_index, momenta_total)
    blocks = green_blocks(sigma_less, sigma_great, hamilton, slab_coupling, energies)
    table_rows = lax.dynamic_slice_in_dim(kz_table, momenta_start, momenta_local, 0)
    weights = momentum_weights(table_rows, mode_weight, momenta_total)
    everyone = lax.all_gather(blocks, "kz", axis=0, tiled=True)
    extended = padded(everyone, (("en", 1),), OFFMAX)
    less_total, great_total = mixed_sums(
        extended, weights, form_factor, occupation, energy_offset, energy_local, OFFMAX
    )
    return (less_total.astype(jnp.bfloat16), great_total.astype(jnp.bfloat16))


def solution(mesh):
    in_specs = (
        P("kz", "en", None, None, None, None),
        P("kz", "en", None, None, None, None),
        P(),
        P(),
        P(),
        P(),
        P(),
        P(),
        P(),
        P(),
        P(),
    )
    out_specs = (P("kz", "en", None, None, None, None), P("kz", "en", None, None, None, None))
    return jax.shard_map(
        on_device, mesh=mesh, in_specs=in_specs, out_specs=out_specs, check_vma=False
    )
```

profile of v0, /device:TPU:63, one launch (start us, length us, event | category | flops | bytes accessed | tf_op | source)
XLA Modules:
  0.0 1277.6 jit_solution(12174855667015090132)
XLA Ops:
  7.4 2.0 fusion.356
  9.4 2.0 fusion.357
  14.7 1.9 fusion.44
  20.6 47.1 %custom-call.23 = f32[1,4,128,128]{3,2,1,0:T(8,128)S(1)} custom-call(f32[1,4,128,128]{3,2,1,0:T(8,128)S(1)} %cholesky.281), custom_call_target="Cholesky" | custom-call | tf_op jit(solution)/shard_map/jit(cholesky)/cholesky | solution.py:62
  67.7 39.3 %custom-call.24 = f32[1,4,1,128,128]{3,4,2,1,0:T(8,128)S(1)} custom-call(f32[1,4,1,128,128]{4,3,2,1,0:T(8,128)S(1)} %select_bitcast_fusion.2), custom_call_target="InvertDiagBlocksLowerTriangular" | custom-call | tf_op jit(solution)/shard_map/jit(cholesky)/cholesky | solution.py:62
  110.1 46.9 %custom-call.25 = f32[1,4,128,128]{3,2,1,0:T(8,128)S(1)} custom-call(f32[1,4,128,128]{3,2,1,0:T(8,128)S(1)} %fusion.25), custom_call_target="Cholesky" | custom-call | tf_op jit(solution)/shard_map/jit(cholesky)/cholesky | solution.py:62
  159.6 4.1 while.6
  163.7 78.8 %custom-call.26 = f32[4,2,128,128]{2,3,1,0:T(8,128)S(1)} custom-call(f32[4,2,128,128]{3,2,1,0:T(8,128)S(1)} %bitcast.917), custom_call_target="InvertDiagBlocksLowerTriangular" | custom-call | tf_op jit(solution)/shard_map/jit(_cho_solve)/vmap()/triangular_solve | solution.py:63
  259.0 47.3 %custom-call.27 = f32[1,4,128,128]{3,2,1,0:T(8,128)S(1)} custom-call(f32[1,4,128,128]{3,2,1,0:T(8,128)S(1)} %cholesky.284), custom_call_target="Cholesky" | custom-call | tf_op jit(solution)/shard_map/jit(cholesky)/cholesky | solution.py:62
  306.4 39.3 %custom-call.28 = f32[1,4,1,128,128]{3,4,2,1,0:T(8,128)S(1)} custom-call(f32[1,4,1,128,128]{4,3,2,1,0:T(8,128)S(1)} %select_bitcast_fusion.1), custom_call_target="InvertDiagBlocksLowerTriangular" | custom-call | tf_op jit(solution)/shard_map/jit(cholesky)/cholesky | solution.py:62
  348.7 46.9 %custom-call.29 = f32[1,4,128,128]{3,2,1,0:T(8,128)S(1)} custom-call(f32[1,4,128,128]{3,2,1,0:T(8,128)S(1)} %fusion.26), custom_call_target="Cholesky" | custom-call | tf_op jit(solution)/shard_map/jit(cholesky)/cholesky | solution.py:62
  396.2 4.1 while.7
  400.3 78.8 %custom-call.30 = f32[4,2,128,128]{2,3,1,0:T(8,128)S(1)} custom-call(f32[4,2,128,128]{3,2,1,0:T(8,128)S(1)} %bitcast.918), custom_call_target="InvertDiagBlocksLowerTriangular" | custom-call | tf_op jit(solution)/shard_map/jit(_cho_solve)/vmap()/triangular_solve | solution.py:63
  479.1 1.9 fusion.53
  497.9 2.1 fusion.40
  510.8 47.3 %custom-call.31 = f32[1,4,128,128]{3,2,1,0:T(8,128)S(1)} custom-call(f32[1,4,128,128]{3,2,1,0:T(8,128)S(1)} %cholesky.287), custom_call_target="Cholesky" | custom-call | tf_op jit(solution)/shard_map/jit(cholesky)/cholesky | solution.py:62
  561.3 40.8 %custom-call.32 = f32[1,4,1,128,128]{3,4,2,1,0:T(8,128)} custom-call(f32[1,4,1,128,128]{4,3,2,1,0:T(8,128)} %select_bitcast_fusion), custom_call_target="InvertDiagBlocksLowerTriangular" | custom-call | tf_op jit(solution)/shard_map/jit(cholesky)/cholesky | solution.py:62
  603.5 2.3 fusion.27
  605.8 48.4 %custom-call.33 = f32[1,4,128,128]{3,2,1,0:T(8,128)} custom-call(f32[1,4,128,128]{3,2,1,0:T(8,128)} %fusion.27), custom_call_target="Cholesky" | custom-call | tf_op jit(solution)/shard_map/jit(cholesky)/cholesky | solution.py:62
  658.6 6.8 while.8
  659.8 2.1 bitcast_dynamic-update-slice_fusion.11
  663.2 2.1 bitcast_dynamic-update-slice_fusion.11
  665.3 80.2 %custom-call.34 = f32[4,2,128,128]{2,3,1,0:T(8,128)} custom-call(f32[4,2,128,128]{3,2,1,0:T(8,128)} %bitcast.916), custom_call_target="InvertDiagBlocksLowerTriangular" | custom-call | tf_op jit(solution)/shard_map/jit(_cho_solve)/vmap()/triangular_solve | solution.py:63
  792.5 2.0 fusion.32
  796.3 2.2 fusion.17
  800.4 2.0 fusion.33
  808.6 2.4 fusion.370
  819.5 2.3 convolution_subtract_fusion.7
  823.6 2.1 fusion.30
  830.1 2.5 fusion.10
  834.4 2.1 fusion.31
  840.0 1.9 convert_bitcast_fusion.2
  847.5 2.1 convert_bitcast_fusion.5
  849.6 2.0 convert_bitcast_fusion.4
  856.0 51.1 %all-gather.2.cloned.1.call-done = bf16[4,4,2,3,2,128,128]{6,5,4,3,2,1,0:T(8,128)(2,1)} async-done(((bf16[1,4,2,3,2,128,128]{6,5,4,3,2,1,0:T(8,128)(2,1)}), bf16[4,4,2,3,2,128,128]{6,5,4,3,2,1,0:T(8,128)(2,1)}) %all-gather.2.cloned.1.call-update) | async-done | bytes 6291472 | tf_op jit(solution)/shard_map/all_gather | solution.py:194
  907.1 2.5 collective-permute-start
  909.6 2.8 collective-permute-start.1
  921.1 125.0 %collective-permute-done = bf16[4,4,2,3,2,128,128]{6,5,4,3,2,1,0:T(8,128)(2,1)} collective-permute-done((bf16[4,4,2,3,2,128,128]{6,5,4,3,2,1,0:T(8,128)(2,1)}, bf16[4,4,2,3,2,128,128]{6,5,4,3,2,1,0:T(8,128)(2,1)}, u32[]{:S(2)}, u32[]{:S(2)}) %collective-permute-start) | collective-permute-done | bytes 6291488 | tf_op jit(solution)/shard_map/ppermute | solution.py:17
  1046.2 8.0 constant_dynamic-update-slice_fusion.2
  1054.2 4.1 constant_dynamic-update-slice_fusion.1
  1058.2 123.7 %collective-permute-done.1 = bf16[4,4,2,3,2,128,128]{6,5,4,3,2,1,0:T(8,128)(2,1)} collective-permute-done((bf16[4,4,2,3,2,128,128]{6,5,4,3,2,1,0:T(8,128)(2,1)}, bf16[4,4,2,3,2,128,128]{6,5,4,3,2,1,0:T(8,128)(2,1)}, u32[]{:S(2)}, u32[]{:S(2)}) %collective-permute-start.1) | collective-permute-done | bytes 6291488 | tf_op jit(solution)/shard_map/ppermute | solution.py:20
  1181.9 8.1 constant_dynamic-update-slice_fusion
  1190.0 18.3 %add_bitcast_fusion.1 = (f32[4,4,3,2,128,128]{5,4,3,2,1,0:T(8,128)S(1)}, f32[4,4,3,2,128,128]{5,4,3,2,1,0:T(8,128)}, f32[4,4,3,2,128,128]{5,4,3,2,1,0:T(8,128)}, f32[4,4,3,2,128,128]{5,4,3,2,1,0:T(8,128)}) fusion(bf16[4,12,2,3,2,128,128]{6,5,4,3,2,1,0:T(8,128)(2,1)} %constant_dynamic-update-slice_fusion, s32[]{:T(128)S(6)} %select_n.19, s32[]{:T(128)S(6)} %add.377, ...), kind=kLoop, calls=%fused_computation.15 | loop fusion | flops 31457280 | bytes 50331684 | tf_op jit(solution)/shard_map/add | solution.py:155
  1208.2 19.0 %fusion.6 = f32[1,4,3,2,128,128]{5,0,4,3,2,1:T(1,128)S(1)} fusion(f32[4,4,3,2,128,128]{5,4,3,2,1,0:T(8,128)} %get-tuple-element.68, f32[2,4]{1,0:T(2,128)S(1)} %fusion.36), kind=kOutput, calls=%fused_computation.12 | convolution fusion | flops 18874368 | bytes 7864832 | tf_op jit(solution)/shard_map/ak,kesrij->aesrij/dot_general | solution.py:158
  1227.2 13.8 %fusion.4 = f32[1,4,3,2,128,128]{5,0,4,3,2,1:T(1,128)S(1)} fusion(f32[4,4,3,2,128,128]{5,4,3,2,1,0:T(8,128)S(1)} %copy-done.3, f32[2,4]{1,0:T(2,128)S(1)} %fusion.36), kind=kOutput, calls=%fused_computation.10 | convolution fusion | flops 18874368 | bytes 7864832 | tf_op jit(solution)/shard_map/ak,kesrij->aesrij/dot_general | solution.py:158
  1241.1 13.6 %fusion.2 = f32[1,4,3,2,128,128]{5,0,4,3,2,1:T(1,128)S(1)} fusion(f32[4,4,3,2,128,128]{5,4,3,2,1,0:T(8,128)S(1)} %get-tuple-element.65, f32[2,4]{1,0:T(2,128)S(1)} %fusion.36), kind=kOutput, calls=%fused_computation.8 | convolution fusion | flops 18874368 | bytes 7864832 | tf_op jit(solution)/shard_map/ak,kesrij->aesrij/dot_general | solution.py:161
  1254.7 13.9 %fusion = f32[1,4,3,2,128,128]{5,0,4,3,2,1:T(1,128)S(1)} fusion(f32[4,4,3,2,128,128]{5,4,3,2,1,0:T(8,128)S(1)} %bitcast.900, f32[2,4]{1,0:T(2,128)S(1)} %fusion.36), kind=kOutput, calls=%fused_computation.6 | convolution fusion | flops 18874368 | bytes 7864832 | tf_op jit(solution)/shard_map/ak,kesrij->aesrij/dot_general | solution.py:161
  1268.6 1.9 fusion.47
  (359 shorter events, 167.9 us)
Async XLA Ops:
  7.2 899.9 %all-gather.2.cloned.1.call-start = ((), (), s32[]{:S(2)}) async-start(), calls=%async_computation | async-start | bytes 7864320 | tf_op jit(solution)/shard_map/all_gather | solution.py:194
  7.3 60.4 %copy-start.56 = (pred[128,128]{1,0:T(8,128)(4,1)}, pred[128,128]{1,0:T(8,128)(4,1)S(1)}, u32[]{:S(2)}) copy-start(pred[128,128]{1,0:T(8,128)(4,1)S(1)} %iota_compare_fusion.1) | copy-start | bytes 49156
  7.4 388.6 %copy-start.36 = (pred[256,256]{1,0:T(8,128)(4,1)}, pred[256,256]{1,0:T(8,128)(4,1)S(1)}, u32[]{:S(2)}) copy-start(pred[256,256]{1,0:T(8,128)(4,1)S(1)} %iota_compare_fusion) | copy-start | bytes 196612
  16.8 233.7 %copy-start.51 = (f32[128,128]{0,1:T(8,128)}, f32[128,128]{0,1:T(8,128)S(1)}, u32[]{:S(2)}) copy-start(f32[128,128]{0,1:T(8,128)S(1)} %copy.266) | copy-start | bytes 196612
  159.6 87.2 %copy-start.2 = (f32[2,128,128]{2,1,0:T(8,128)S(1)}, f32[2,128,128]{2,1,0:T(8,128)}, u32[]{:S(2)}) copy-start(f32[2,128,128]{2,1,0:T(8,128)} %param.18) | copy-start | bytes 393220
  163.7 83.7 %copy-start.63 = (s32[2,2]{1,0:T(2,128)}, s32[2,2]{1,0:T(2,128)S(1)}, u32[]{:S(2)}) copy-start(s32[2,2]{1,0:T(2,128)S(1)} %get-tuple-element.256) | copy-start | bytes 52
  248.1 8.5 copy-start.52
  251.9 54.4 %copy-start.57 = (pred[128,128]{1,0:T(8,128)(4,1)S(1)}, pred[128,128]{1,0:T(8,128)(4,1)}, u32[]{:S(2)}) copy-start(pred[128,128]{1,0:T(8,128)(4,1)} %copy-done.56) | copy-start | bytes 49156
  255.2 140.9 %copy-start.64 = (s32[2,2]{1,0:T(2,128)S(1)}, s32[2,2]{1,0:T(2,128)}, u32[]{:S(2)}) copy-start(s32[2,2]{1,0:T(2,128)} %copy-done.63) | copy-start | bytes 52
  479.1 11.8 copy-start.50
  489.7 13.0 %copy-start.40 = (bf16[1,4,2,128,128]{4,3,1,2,0:T(8,128)(2,1)S(1)}, bf16[1,4,2,128,128]{4,3,1,2,0:T(8,128)(2,1)}, u32[]{:S(2)}) copy-start(bf16[1,4,2,128,128]{4,3,1,2,0:T(8,128)(2,1)} %get-tuple-element.88) | copy-start | bytes 786436
  492.7 12.7 copy-start.29
  745.6 8.9 copy-start.41
  745.6 8.9 copy-start.47
  754.8 8.8 copy-start.30
  755.5 12.4 copy-start.8
  757.6 26.9 %copy-start.10 = (f32[4,128,128]{1,2,0:T(8,128)}, f32[4,128,128]{1,2,0:T(8,128)S(1)}, u32[]{:S(2)}) copy-start(f32[4,128,128]{1,2,0:T(8,128)S(1)} %convolution_subtract_fusion.24) | copy-start | bytes 786436
  759.8 9.2 copy-start.19
  762.5 9.3 copy-start.18
  763.1 25.7 %copy-start.15 = (f32[4,128,128]{1,2,0:T(8,128)}, f32[4,128,128]{1,2,0:T(8,128)S(1)}, u32[]{:S(2)}) copy-start(f32[4,128,128]{1,2,0:T(8,128)S(1)} %convolution_add_fusion.13) | copy-start | bytes 786436
  768.9 13.7 %copy-start.4 = (f32[4,128,128]{2,1,0:T(8,128)}, f32[4,128,128]{2,1,0:T(8,128)S(1)}, u32[]{:S(2)}) copy-start(f32[4,128,128]{2,1,0:T(8,128)S(1)} %fusion.174) | copy-start | bytes 786436
  773.1 10.6 copy-start.16
  774.2 10.4 copy-start.20
  779.8 9.1 copy-start.24
  783.7 11.5 copy-start.5
  800.3 10.7 copy-start.7
  800.3 11.8 copy-start.13
  800.4 11.8 copy-start.34
  802.4 9.8 copy-start.35
  802.4 13.1 %copy-start.17 = (f32[4,128,128]{2,1,0:T(8,128)S(1)}, f32[4,128,128]{2,1,0:T(8,128)}, u32[]{:S(2)}) copy-start(f32[4,128,128]{2,1,0:T(8,128)} %copy-done.16) | copy-start | bytes 786436
  802.4 14.6 %copy-start.14 = (f32[1,4,128,128]{3,2,1,0:T(8,128)S(1)}, f32[1,4,128,128]{3,2,1,0:T(8,128)}, u32[]{:S(2)}) copy-start(f32[1,4,128,128]{3,2,1,0:T(8,128)} %copy-done.12) | copy-start | bytes 786436
  802.4 17.1 %copy-start.9 = (f32[4,128,128]{1,2,0:T(8,128)S(1)}, f32[4,128,128]{1,2,0:T(8,128)}, u32[]{:S(2)}) copy-start(f32[4,128,128]{1,2,0:T(8,128)} %copy-done.8) | copy-start | bytes 786436
  803.8 11.0 copy-start.21
  807.3 22.9 %copy-start.11 = (f32[4,128,128]{1,2,0:T(8,128)S(1)}, f32[4,128,128]{1,2,0:T(8,128)}, u32[]{:S(2)}) copy-start(f32[4,128,128]{1,2,0:T(8,128)} %copy-done.10) | copy-start | bytes 786436
  817.0 23.0 %copy-start.23 = (f32[1,4,128,128]{3,2,1,0:T(8,128)S(1)}, f32[1,4,128,128]{3,2,1,0:T(8,128)}, u32[]{:S(2)}) copy-start(f32[1,4,128,128]{3,2,1,0:T(8,128)} %copy-done.22) | copy-start | bytes 786436
  830.1 22.6 %copy-start.53 = (bf16[1,4,1,128,128]{3,4,1,2,0:T(8,128)(2,1)S(1)}, bf16[1,4,1,128,128]{3,4,1,2,0:T(8,128)(2,1)}, u32[]{:S(2)}) copy-start(bf16[1,4,1,128,128]{3,4,1,2,0:T(8,128)(2,1)} %convert_bitcast_fusion) | copy-start | bytes 393220
  853.7 58.7 %copy-start.60 = (s32[2]{0:T(128)S(1)}, s32[2]{0:T(128)}, u32[]{:S(2)}) copy-start(s32[2]{0:T(128)} %param.24) | copy-start | bytes 28
  853.7 64.5 %copy-start.61 = (f32[2]{0:T(128)S(1)}, f32[2]{0:T(128)}, u32[]{:S(2)}) copy-start(f32[2]{0:T(128)} %param.23) | copy-start | bytes 28
  853.7 67.2 %copy-start.62 = (f32[2,4]{1,0:T(2,128)S(1)}, f32[2,4]{1,0:T(2,128)}, u32[]{:S(2)}) copy-start(f32[2,4]{1,0:T(2,128)} %param.21) | copy-start | bytes 100
  853.8 67.3 %copy-start.58 = (f32[2,128,128]{2,1,0:T(8,128)S(1)}, f32[2,128,128]{2,1,0:T(8,128)}, u32[]{:S(2)}) copy-start(f32[2,128,128]{2,1,0:T(8,128)} %param.22) | copy-start | bytes 393220
  907.1 139.1 %collective-permute-start = (bf16[4,4,2,3,2,128,128]{6,5,4,3,2,1,0:T(8,128)(2,1)}, bf16[4,4,2,3,2,128,128]{6,5,4,3,2,1,0:T(8,128)(2,1)}, u32[]{:S(2)}, u32[]{:S(2)}) collective-permute-start(bf16[4,4,2,3,2,128,128]{6,5,4,3,2,1,0:T(8,128)(2,1)} %all-gather.2.cloned.1.call-done), channel_id=1, source_target_pairs={{0,1},{1,2},{2,3},{3,4},{4,5},{5,6},{6,7},{7,8},{8,9},{9,10},{10,1... | collective-permute-start | bytes 18874376 | tf_op jit(solution)/shard_map/ppermute | solution.py:17
  909.6 272.3 %collective-permute-start.1 = (bf16[4,4,2,3,2,128,128]{6,5,4,3,2,1,0:T(8,128)(2,1)}, bf16[4,4,2,3,2,128,128]{6,5,4,3,2,1,0:T(8,128)(2,1)}, u32[]{:S(2)}, u32[]{:S(2)}) collective-permute-start(bf16[4,4,2,3,2,128,128]{6,5,4,3,2,1,0:T(8,128)(2,1)} %all-gather.2.cloned.1.call-done), channel_id=1, source_target_pairs={{1,0},{2,1},{3,2},{4,3},{5,4},{6,5},{7,6},{8,7},{9,8},{10,9},{11,1... | collective-permute-start | bytes 18874376 | tf_op jit(solution)/shard_map/ppermute | solution.py:20
  921.1 133.1 %slice-start.2 = ((s8[6291456]{0:T(1024)(128)(4,1)}), s8[4194304]{0:T(1024)(128)(4,1)S(1)}, s32[]{:S(2)}) async-start(s8[6291456]{0:T(1024)(128)(4,1)} %bitcast.901), calls=%async_computation.3 | async-start | bytes 8388608
  921.1 133.1 %slice-start.3 = ((s8[6291456]{0:T(1024)(128)(4,1)}), s8[2097152]{0:T(1024)(128)(4,1)S(1)}, s32[]{:S(2)}) async-start(s8[6291456]{0:T(1024)(128)(4,1)} %bitcast.901), calls=%async_computation.4 | async-start | bytes 4194304
  1208.2 19.0 %copy-start.3 = (f32[4,4,3,2,128,128]{5,4,3,2,1,0:T(8,128)S(1)}, f32[4,4,3,2,128,128]{5,4,3,2,1,0:T(8,128)}, u32[]{:S(2)}) copy-start(f32[4,4,3,2,128,128]{5,4,3,2,1,0:T(8,128)} %get-tuple-element.66) | copy-start | bytes 18874372
  1227.2 27.5 %slice-start = ((s8[6291456]{0:T(1024)(128)(4,1)}), s8[4194304]{0:T(1024)(128)(4,1)S(1)}, s32[]{:S(2)}) async-start(s8[6291456]{0:T(1024)(128)(4,1)} %bitcast.899), calls=%async_computation.1 | async-start | bytes 8388608
  1241.1 13.6 %slice-start.1 = ((s8[6291456]{0:T(1024)(128)(4,1)}), s8[2097152]{0:T(1024)(128)(4,1)S(1)}, s32[]{:S(2)}) async-start(s8[6291456]{0:T(1024)(128)(4,1)} %bitcast.899), calls=%async_computation.2 | async-start | bytes 4194304
  1254.7 15.8 %copy-start.1 = (f32[3,128,128]{2,1,0:T(8,128)S(1)}, f32[3,128,128]{2,1,0:T(8,128)}, u32[]{:S(2)}) copy-start(f32[3,128,128]{2,1,0:T(8,128)} %param.16) | copy-start | bytes 589828
  (24 other events, 91.2 us)
Sparse Core Ops, SparseCore 0:
  856.1 50.9 all-gather.1
where the time goes:
time: 1290 us; the launch traced here: 1280 us
  other arithmetic  685 us (53%)
  waiting for transfers between devices  300 us (23%)
  matrix products  181 us (14%)
  local copies, waits for them, and re-layouts  83.6 us (6%)
  between operations  22.8 us (2%)
    another operation x26, other arithmetic, invert_pair(): factor = jnp.linalg.cholesky(normal)  407 us
    another operation x8, other arithmetic, invert_pair(): solved = jax.scipy.linalg.cho_solve((factor, True), transposed)  241 us
    ppermute x1, waiting for transfers between devices, padded(): lax.ppermute(lax.slice_in_dim(block, block.shape[dim] - width, None, axis...  125 us
    ppermute x1, waiting for transfers between devices, padded(): lax.ppermute(lax.slice_in_dim(block, 0, width, axis=dim), axis, backward)  124 us
    dot_general x95, matrix products, matmul_high(): jnp.matmul(left_matrix, right_matrix, precision=lax.Precision.HIGHEST)  89.9 us
    all_gather x1, waiting for transfers between devices, on_device(): everyone = lax.all_gather(blocks, 'kz', axis=0, tiled=True)  51.1 us
    dot_general x2, matrix products, mixed_sums(): jnp.einsum('ak,kesrij->aesrij', weights[mode_index], less_term, precision...  32.8 us
    dot_general x2, matrix products, mixed_sums(): jnp.einsum('ak,kesrij->aesrij', weights[mode_index], great_term, precisio...  27.5 us
  transfers between devices with their start and end apart: 3, of which 3 were waited for; matrix products, arithmetic and copies ran while one was open for 1% of the time, Pallas kernels for 0%

commit v1 on v0

--- a/solution.py
+++ b/solution.py
@@ -2,6 +2,7 @@
 import jax.numpy as jnp
 from jax import lax
 from jax.sharding import PartitionSpec as P
+from jax.experimental import pallas as pl
 
 OFFMAX = 4
 
@@ -52,16 +53,61 @@
     return (left_pair[0] - right_pair[0], left_pair[1] - right_pair[1])
 
 
-def invert_pair(pair_value):
-    orbitals = pair_value[0].shape[-1]
-    upper_half = jnp.concatenate([pair_value[0], -pair_value[1]], axis=-1)
-    lower_half = jnp.concatenate([pair_value[1], pair_value[0]], axis=-1)
-    embedded = jnp.concatenate([upper_half, lower_half], axis=-2)
-    transposed = jnp.swapaxes(embedded, -1, -2)
-    normal = matmul_high(transposed, embedded)
-    factor = jnp.linalg.cholesky(normal)
-    solved = jax.scipy.linalg.cho_solve((factor, True), transposed)
-    return (solved[..., :orbitals, :orbitals], solved[..., orbitals:, :orbitals])
+def sweep_kernel(normal_re_ref, normal_im_ref, out_re_ref, out_im_ref):
+    batch, orbitals, _ = normal_re_ref.shape
+    out_re_ref[...] = normal_re_ref[...]
+    out_im_ref[...] = normal_im_ref[...]
+    lane = lax.broadcasted_iota(jnp.int32, (1, orbitals), 1)
+    row_index = lax.broadcasted_iota(jnp.int32, (orbitals, 1), 0)
+
+    def step(pivot, carry):
+        lane_hit = lane == pivot
+        row_hit = row_index == pivot
+        for item in range(batch):
+            whole_re = out_re_ref[item]
+            whole_im = out_im_ref[item]
+            row_re = out_re_ref[item, pl.ds(pivot, 1), :]
+            row_im = out_im_ref[item, pl.ds(pivot, 1), :]
+            col_re = jnp.sum(jnp.where(lane_hit, whole_re, 0.0), axis=1, keepdims=True)
+            col_im = jnp.sum(jnp.where(lane_hit, whole_im, 0.0), axis=1, keepdims=True)
+            piv_re = jnp.sum(jnp.where(lane_hit, row_re, 0.0), axis=1, keepdims=True)
+            piv_im = jnp.sum(jnp.where(lane_hit, row_im, 0.0), axis=1, keepdims=True)
+            norm = piv_re * piv_re + piv_im * piv_im
+            inv_re = piv_re / norm
+            inv_im = -piv_im / norm
+            scaled_re = jnp.where(lane_hit, inv_re, row_re * inv_re - row_im * inv_im)
+            scaled_im = jnp.where(lane_hit, inv_im, row_re * inv_im + row_im * inv_re)
+            col_re = jnp.where(row_hit, 0.0, col_re)
+            col_im = jnp.where(row_hit, 0.0, col_im)
+            base_re = jnp.where(lane_hit, 0.0, whole_re)
+            base_im = jnp.where(lane_hit, 0.0, whole_im)
+            out_re_ref[item] = base_re - (col_re * scaled_re - col_im * scaled_im)
+            out_im_ref[item] = base_im - (col_re * scaled_im + col_im * scaled_re)
+            out_re_ref[item, pl.ds(pivot, 1), :] = scaled_re
+            out_im_ref[item, pl.ds(pivot, 1), :] = scaled_im
+        return carry
+
+    lax.fori_loop(0, orbitals, step, 0)
+
+
+def hermitian_inverse(normal_pair, interpret=False):
+    shape = normal_pair[0].shape
+    orbitals = shape[-1]
+    flat = [item.reshape(-1, orbitals, orbitals) for item in normal_pair]
+    out_shape = jax.ShapeDtypeStruct(flat[0].shape, jnp.float32)
+    inverse = pl.pallas_call(
+        sweep_kernel,
+        out_shape=(out_shape, out_shape),
+        interpret=interpret,
+    )(*flat)
+    return (inverse[0].reshape(shape), inverse[1].reshape(shape))
+
+
+def invert_pair(pair_value, interpret=False):
+    adjoint_value = adjoint(pair_value)
+    normal = complex_product(adjoint_value, pair_value)
+    normal_inverse = hermitian_inverse(normal, interpret)
+    return complex_product(normal_inverse, adjoint_value)
 
 
 def greater_of(less_pair, ret_pair):

time: 1290 us -> 774 us (0.60)
  other arithmetic: 685 us -> 28.1 us
  Pallas kernels: 0 us -> 191 us
  local copies, waits for them, and re-layouts: 83.6 us -> 46.6 us
  matrix products: 181 us -> 168 us
    another operation x34 -> x0, other arithmetic: 648 us -> none  [the longest x26 407 us: invert_pair(): factor = jnp.linalg.cholesky(normal)]
    pallas_call x0 -> x3, Pallas kernels: none -> 191 us  [hermitian_inverse(): pl.pallas_call(sweep_kernel, out_shape=(out_shape, out_shape), interpret=...]
    another operation x24 -> x0, matrix products: 29.6 us -> none  [the longest x18 19.9 us: invert_pair(): solved = jax.scipy.linalg.cho_solve((factor, True), transposed)]
    another operation x28 -> x0, local copies, waits for them, and re-layouts: 17 us -> none  [the longest x22 15.8 us: invert_pair(): solved = jax.scipy.linalg.cho_solve((factor, True), transposed)]
    dot_general x95 -> x116, matrix products: 89.9 us -> 106 us  [matmul_high(): jnp.matmul(left_matrix, right_matrix, precision=lax.Precision.HIGHEST)]
  transfers between devices with their start and end apart: 3 -> 3, of which waited for: 3 -> 3; matrix products, arithmetic and copies ran while one was open for 1% -> 2% of each run, Pallas kernels for 0% -> 0%
where the time goes in v1:
time: 774 us; the launch traced here: 762 us
  waiting for transfers between devices  300 us (39%)
  Pallas kernels  191 us (25%)
  matrix products  168 us (22%)
  local copies, waits for them, and re-layouts  46.6 us (6%)
  other arithmetic  28.1 us (4%)
  between operations  22.7 us (3%)
    pallas_call x3, Pallas kernels, hermitian_inverse(): pl.pallas_call(sweep_kernel, out_shape=(out_shape, out_shape), interpret=...  191 us
    ppermute x1, waiting for transfers between devices, padded(): lax.ppermute(lax.slice_in_dim(block, block.shape[dim] - width, None, axis...  125 us
    ppermute x1, waiting for transfers between devices, padded(): lax.ppermute(lax.slice_in_dim(block, 0, width, axis=dim), axis, backward)  124 us
    dot_general x116, matrix products, matmul_high(): jnp.matmul(left_matrix, right_matrix, precision=lax.Precision.HIGHEST)  106 us
    all_gather x1, waiting for transfers between devices, on_device(): everyone = lax.all_gather(blocks, 'kz', axis=0, tiled=True)  51.1 us
    dot_general x2, matrix products, mixed_sums(): jnp.einsum('ak,kesrij->aesrij', weights[mode_index], less_term, precision...  32.8 us
    dot_general x2, matrix products, mixed_sums(): jnp.einsum('ak,kesrij->aesrij', weights[mode_index], great_term, precisio...  27.5 us
    add x1, other arithmetic, mixed_sums(): (occupied + 1.0) * lower_side[:, :, 1].astype(jnp.float32)  18.2 us
  transfers between devices with their start and end apart: 3, of which 3 were waited for; matrix products, arithmetic and copies ran while one was open for 2% of the time, Pallas kernels for 0%

profile of v1, /device:TPU:63, one launch (start us, length us, event | category | flops | bytes accessed | tf_op | source)
XLA Modules:
  0.0 761.9 jit_solution(12928976205662987149)
XLA Ops:
  7.3 2.0 fusion.267
  9.2 1.9 fusion.268
  17.1 63.7 %shard_map.122 = (f32[4,128,128]{2,1,0:T(8,128)}, f32[4,128,128]{2,1,0:T(8,128)}) custom-call(f32[4,128,128]{2,1,0:T(8,128)} %convolution_subtract_fusion.25.normal_re_ref, f32[4,128,128]{2,1,0:T(8,128)} %convolution_add_fusion.25.normal_im_ref), custom_call_target="tpu_custom_call" | custom-call | tf_op jit(solution)/shard_map/pallas_call | solution.py:98
  80.8 1.6 fusion.127
  82.5 1.7 fusion.133
  84.1 1.7 convolution_add_fusion.24
  85.8 1.6 convolution_subtract_fusion.24
  95.8 63.7 %shard_map.123 = (f32[4,128,128]{2,1,0:T(8,128)}, f32[4,128,128]{2,1,0:T(8,128)}) custom-call(f32[4,128,128]{2,1,0:T(8,128)} %convolution_subtract_fusion.19.normal_re_ref, f32[4,128,128]{2,1,0:T(8,128)} %convolution_add_fusion.22.normal_im_ref), custom_call_target="tpu_custom_call" | custom-call | tf_op jit(solution)/shard_map/pallas_call | solution.py:98
  159.5 1.6 fusion.118
  161.1 1.6 fusion.39
  162.7 1.6 convolution_subtract_fusion.18
  165.3 1.6 convolution_add_fusion.20
  174.4 63.7 %shard_map.124 = (f32[4,128,128]{2,1,0:T(8,128)}, f32[4,128,128]{2,1,0:T(8,128)}) custom-call(f32[4,128,128]{2,1,0:T(8,128)} %convolution_subtract_fusion.13.normal_re_ref, f32[4,128,128]{2,1,0:T(8,128)} %convolution_add_fusion.16.normal_im_ref), custom_call_target="tpu_custom_call" | custom-call | tf_op jit(solution)/shard_map/pallas_call | solution.py:98
  238.2 1.7 fusion.32
  239.9 1.6 fusion.97
  279.8 1.8 copy.182
  283.5 2.0 fusion.24
  287.3 2.2 fusion.18
  289.5 1.8 copy.188
  291.3 2.0 fusion.25
  294.7 1.7 convolution_subtract_fusion.5
  306.8 2.3 convolution_subtract_fusion.1
  309.2 1.8 copy.195
  310.9 2.1 fusion.10
  313.0 1.8 copy.205
  316.6 2.3 fusion.11
  318.9 1.8 copy.202
  320.7 2.1 fusion.9
  322.8 1.9 copy.206
  324.6 1.7 copy.203
  327.1 1.7 convert_bitcast_fusion.2
  328.8 1.7 copy.204
  333.9 1.9 convert_bitcast_fusion.5
  335.8 1.9 convert_bitcast_fusion.4
  340.1 51.1 %all-gather.2.cloned.1.call-done = bf16[4,4,2,3,2,128,128]{6,5,4,3,2,1,0:T(8,128)(2,1)} async-done(((bf16[1,4,2,3,2,128,128]{6,5,4,3,2,1,0:T(8,128)(2,1)}), bf16[4,4,2,3,2,128,128]{6,5,4,3,2,1,0:T(8,128)(2,1)}) %all-gather.2.cloned.1.call-update) | async-done | bytes 6291472 | tf_op jit(solution)/shard_map/all_gather | solution.py:240
  391.3 2.5 collective-permute-start
  393.8 2.8 collective-permute-start.1
  405.3 125.0 %collective-permute-done = bf16[4,4,2,3,2,128,128]{6,5,4,3,2,1,0:T(8,128)(2,1)} collective-permute-done((bf16[4,4,2,3,2,128,128]{6,5,4,3,2,1,0:T(8,128)(2,1)}, bf16[4,4,2,3,2,128,128]{6,5,4,3,2,1,0:T(8,128)(2,1)}, u32[]{:S(2)}, u32[]{:S(2)}) %collective-permute-start) | collective-permute-done | bytes 6291488 | tf_op jit(solution)/shard_map/ppermute | solution.py:18
  530.3 8.0 %constant_dynamic-update-slice_fusion.2 = bf16[4,12,2,3,2,128,128]{6,5,4,3,2,1,0:T(8,128)(2,1)} fusion(bf16[4,4,2,3,2,128,128]{6,5,4,3,2,1,0:T(8,128)(2,1)} %collective-permute-done), kind=kLoop, calls=%fused_computation.374 | loop fusion | bytes 12582912
  538.3 4.1 constant_dynamic-update-slice_fusion.1
  542.4 123.6 %collective-permute-done.1 = bf16[4,4,2,3,2,128,128]{6,5,4,3,2,1,0:T(8,128)(2,1)} collective-permute-done((bf16[4,4,2,3,2,128,128]{6,5,4,3,2,1,0:T(8,128)(2,1)}, bf16[4,4,2,3,2,128,128]{6,5,4,3,2,1,0:T(8,128)(2,1)}, u32[]{:S(2)}, u32[]{:S(2)}) %collective-permute-start.1) | collective-permute-done | bytes 6291488 | tf_op jit(solution)/shard_map/ppermute | solution.py:21
  666.1 8.1 %constant_dynamic-update-slice_fusion = bf16[4,12,2,3,2,128,128]{6,5,4,3,2,1,0:T(8,128)(2,1)} fusion(bf16[4,12,2,3,2,128,128]{6,5,4,3,2,1,0:T(8,128)(2,1)} %constant_dynamic-update-slice_fusion.1, bf16[4,4,2,3,2,128,128]{6,5,4,3,2,1,0:T(8,128)(2,1)} %collective-permute-done.1), kind=kLoop, calls=%fused_computation.372 | loop fusion | bytes 12582912 | tf_op jit(solution)/shard_map/concatenate | solution.py:22
  674.2 18.2 %add_bitcast_fusion.1 = (f32[4,4,3,2,128,128]{5,4,3,2,1,0:T(8,128)S(1)}, f32[4,4,3,2,128,128]{5,4,3,2,1,0:T(8,128)}, f32[4,4,3,2,128,128]{5,4,3,2,1,0:T(8,128)}, f32[4,4,3,2,128,128]{5,4,3,2,1,0:T(8,128)}) fusion(bf16[4,12,2,3,2,128,128]{6,5,4,3,2,1,0:T(8,128)(2,1)} %constant_dynamic-update-slice_fusion, s32[]{:T(128)S(6)} %select_n.16, s32[]{:T(128)S(6)} %add.390, ...), kind=kLoop, calls=%fused_computation.9 | loop fusion | flops 31457280 | bytes 50331684 | tf_op jit(solution)/shard_map/add | solution.py:201
  692.4 19.0 %fusion.6 = f32[1,4,3,2,128,128]{5,0,4,3,2,1:T(1,128)S(1)} fusion(f32[4,4,3,2,128,128]{5,4,3,2,1,0:T(8,128)} %get-tuple-element.17, f32[2,4]{1,0:T(2,128)S(1)} %fusion.28), kind=kOutput, calls=%fused_computation.6 | convolution fusion | flops 18874368 | bytes 7864832 | tf_op jit(solution)/shard_map/ak,kesrij->aesrij/dot_general | solution.py:204
  711.4 13.8 %fusion.4 = f32[1,4,3,2,128,128]{5,0,4,3,2,1:T(1,128)S(1)} fusion(f32[4,4,3,2,128,128]{5,4,3,2,1,0:T(8,128)S(1)} %copy-done.3, f32[2,4]{1,0:T(2,128)S(1)} %fusion.28), kind=kOutput, calls=%fused_computation.4 | convolution fusion | flops 18874368 | bytes 7864832 | tf_op jit(solution)/shard_map/ak,kesrij->aesrij/dot_general | solution.py:204
  725.2 13.6 %fusion.2 = f32[1,4,3,2,128,128]{5,0,4,3,2,1:T(1,128)S(1)} fusion(f32[4,4,3,2,128,128]{5,4,3,2,1,0:T(8,128)S(1)} %get-tuple-element.14, f32[2,4]{1,0:T(2,128)S(1)} %fusion.28), kind=kOutput, calls=%fused_computation.2 | convolution fusion | flops 18874368 | bytes 7864832 | tf_op jit(solution)/shard_map/ak,kesrij->aesrij/dot_general | solution.py:207
  738.9 13.9 %fusion = f32[1,4,3,2,128,128]{5,0,4,3,2,1:T(1,128)S(1)} fusion(f32[4,4,3,2,128,128]{5,4,3,2,1,0:T(8,128)S(1)} %bitcast.776, f32[2,4]{1,0:T(2,128)S(1)} %fusion.28), kind=kOutput, calls=%fused_computation | convolution fusion | flops 18874368 | bytes 7864832 | tf_op jit(solution)/shard_map/ak,kesrij->aesrij/dot_general | solution.py:207
  752.7 1.9 fusion.30
  (208 shorter events, 85.8 us)
Async XLA Ops:
  7.2 4.1 copy-start
  7.2 384.1 %all-gather.2.cloned.1.call-start = ((), (), s32[]{:S(2)}) async-start(), calls=%async_computation | async-start | bytes 7864320 | tf_op jit(solution)/shard_map/all_gather | solution.py:240
  12.8 74.6 %copy-start.2 = (f32[2,128,128]{2,1,0:T(8,128)S(1)}, f32[2,128,128]{2,1,0:T(8,128)}, u32[]{:S(2)}) copy-start(f32[2,128,128]{2,1,0:T(8,128)} %param.15) | copy-start | bytes 393220
  13.1 76.7 %copy-start.22 = (bf16[1,4,1,2,128,128]{5,4,3,2,1,0:T(8,128)(2,1)S(1)}, bf16[1,4,1,2,128,128]{5,4,3,2,1,0:T(8,128)(2,1)}, u32[]{:S(2)}) copy-start(bf16[1,4,1,2,128,128]{5,4,3,2,1,0:T(8,128)(2,1)} %get-tuple-element.24) | copy-start | bytes 786436
  89.7 1.6 copy-start.10
  238.2 10.1 %copy-start.11 = (f32[1,4,2,128,128]{4,3,1,2,0:T(8,128)S(1)}, f32[1,4,2,128,128]{4,3,1,2,0:T(8,128)}, u32[]{:S(2)}) copy-start(f32[1,4,2,128,128]{4,3,1,2,0:T(8,128)} %copy-done.10) | copy-start | bytes 1572868
  241.8 29.7 %copy-start.7 = (f32[4,128,128]{2,1,0:T(8,128)}, f32[4,128,128]{2,1,0:T(8,128)S(1)}, u32[]{:S(2)}) copy-start(f32[4,128,128]{2,1,0:T(8,128)S(1)} %fusion.191) | copy-start | bytes 786436
  242.4 8.7 %copy-start.23 = (f32[4,128,128]{2,1,0:T(8,128)S(1)}, f32[4,128,128]{2,1,0:T(8,128)}, u32[]{:S(2)}) copy-start(f32[4,128,128]{2,1,0:T(8,128)} %get-tuple-element.13) | copy-start | bytes 786436
  254.3 25.5 %copy-start.5 = (f32[4,128,128]{2,1,0:T(8,128)}, f32[4,128,128]{2,1,0:T(8,128)S(1)}, u32[]{:S(2)}) copy-start(f32[4,128,128]{2,1,0:T(8,128)S(1)} %convolution_subtract_fusion.16) | copy-start | bytes 786436
  255.0 23.4 %copy-start.4 = (f32[4,128,128]{1,2,0:T(8,128)}, f32[4,128,128]{1,2,0:T(8,128)S(1)}, u32[]{:S(2)}) copy-start(f32[4,128,128]{1,2,0:T(8,128)S(1)} %convolution_add_fusion.13) | copy-start | bytes 786436
  264.2 9.5 %copy-start.15 = (f32[4,128,128]{2,1,0:T(8,128)}, f32[4,128,128]{2,1,0:T(8,128)S(1)}, u32[]{:S(2)}) copy-start(f32[4,128,128]{2,1,0:T(8,128)S(1)} %convolution_subtract_fusion.10) | copy-start | bytes 786436
  270.8 4.0 copy-start.8
  272.4 7.4 copy-start.6
  283.5 3.8 copy-start.21
  285.5 0.7 copy-start.12
  286.2 18.9 %copy-start.9 = (f32[4,128,128]{2,1,0:T(8,128)S(1)}, f32[4,128,128]{2,1,0:T(8,128)}, u32[]{:S(2)}) copy-start(f32[4,128,128]{2,1,0:T(8,128)} %copy-done.8) | copy-start | bytes 786436
  291.3 10.7 %copy-start.13 = (f32[1,4,128,128]{3,2,1,0:T(8,128)S(1)}, f32[1,4,128,128]{3,2,1,0:T(8,128)}, u32[]{:S(2)}) copy-start(f32[1,4,128,128]{3,2,1,0:T(8,128)} %copy-done.12) | copy-start | bytes 786436
  291.3 11.5 %copy-start.16 = (f32[4,128,128]{2,1,0:T(8,128)S(1)}, f32[4,128,128]{2,1,0:T(8,128)}, u32[]{:S(2)}) copy-start(f32[4,128,128]{2,1,0:T(8,128)} %copy-done.15) | copy-start | bytes 786436
  293.3 10.3 %copy-start.17 = (f32[1,4,128,128]{2,3,1,0:T(8,128)}, f32[1,4,128,128]{2,3,1,0:T(8,128)S(1)}, u32[]{:S(2)}) copy-start(f32[1,4,128,128]{2,3,1,0:T(8,128)S(1)} %fusion.25) | copy-start | bytes 786436
  294.7 20.1 %copy-start.14 = (f32[1,4,128,128]{3,2,1,0:T(8,128)S(1)}, f32[1,4,128,128]{3,2,1,0:T(8,128)}, u32[]{:S(2)}) copy-start(f32[1,4,128,128]{3,2,1,0:T(8,128)} %copy-done.12) | copy-start | bytes 786436
  304.3 22.9 %copy-start.18 = (f32[1,4,128,128]{2,3,1,0:T(8,128)S(1)}, f32[1,4,128,128]{2,3,1,0:T(8,128)}, u32[]{:S(2)}) copy-start(f32[1,4,128,128]{2,3,1,0:T(8,128)} %copy-done.17) | copy-start | bytes 786436
  316.2 17.7 %copy-start.19 = (f32[4,128,128]{2,1,0:T(8,128)S(1)}, f32[4,128,128]{2,1,0:T(8,128)}, u32[]{:S(2)}) copy-start(f32[4,128,128]{2,1,0:T(8,128)} %fusion.10) | copy-start | bytes 786436
  320.7 17.1 %copy-start.24 = (bf16[1,4,1,128,128]{3,4,1,2,0:T(8,128)(2,1)S(1)}, bf16[1,4,1,128,128]{3,4,1,2,0:T(8,128)(2,1)}, u32[]{:S(2)}) copy-start(bf16[1,4,1,128,128]{3,4,1,2,0:T(8,128)(2,1)} %convert_bitcast_fusion) | copy-start | bytes 393220
  322.8 13.0 %copy-start.20 = (f32[1,4,128,128]{3,2,1,0:T(8,128)S(1)}, f32[1,4,128,128]{3,2,1,0:T(8,128)}, u32[]{:S(2)}) copy-start(f32[1,4,128,128]{3,2,1,0:T(8,128)} %fusion.9) | copy-start | bytes 786436
  328.8 8.9 %copy-start.25 = (bf16[1,4,1,128,128]{3,4,1,2,0:T(8,128)(2,1)S(1)}, bf16[1,4,1,128,128]{3,4,1,2,0:T(8,128)(2,1)}, u32[]{:S(2)}) copy-start(bf16[1,4,1,128,128]{3,4,1,2,0:T(8,128)(2,1)} %copy.203) | copy-start | bytes 393220
  332.7 5.0 copy-start.28
  332.7 5.1 copy-start.26
  332.7 5.2 copy-start.27
  337.8 58.7 %copy-start.30 = (s32[2]{0:T(128)S(1)}, s32[2]{0:T(128)}, u32[]{:S(2)}) copy-start(s32[2]{0:T(128)} %param.21) | copy-start | bytes 28
  337.8 64.5 %copy-start.31 = (f32[2]{0:T(128)S(1)}, f32[2]{0:T(128)}, u32[]{:S(2)}) copy-start(f32[2]{0:T(128)} %param.20) | copy-start | bytes 28
  337.9 67.2 %copy-start.32 = (f32[2,4]{1,0:T(2,128)S(1)}, f32[2,4]{1,0:T(2,128)}, u32[]{:S(2)}) copy-start(f32[2,4]{1,0:T(2,128)} %param.18) | copy-start | bytes 100
  337.9 67.4 %copy-start.29 = (f32[2,128,128]{2,1,0:T(8,128)S(1)}, f32[2,128,128]{2,1,0:T(8,128)}, u32[]{:S(2)}) copy-start(f32[2,128,128]{2,1,0:T(8,128)} %param.19) | copy-start | bytes 393220
  391.3 139.1 %collective-permute-start = (bf16[4,4,2,3,2,128,128]{6,5,4,3,2,1,0:T(8,128)(2,1)}, bf16[4,4,2,3,2,128,128]{6,5,4,3,2,1,0:T(8,128)(2,1)}, u32[]{:S(2)}, u32[]{:S(2)}) collective-permute-start(bf16[4,4,2,3,2,128,128]{6,5,4,3,2,1,0:T(8,128)(2,1)} %all-gather.2.cloned.1.call-done), channel_id=1, source_target_pairs={{0,1},{1,2},{2,3},{3,4},{4,5},{5,6},{6,7},{7,8},{8,9},{9,10},{10,1... | collective-permute-start | bytes 18874376 | tf_op jit(solution)/shard_map/ppermute | solution.py:18
  393.8 272.3 %collective-permute-start.1 = (bf16[4,4,2,3,2,128,128]{6,5,4,3,2,1,0:T(8,128)(2,1)}, bf16[4,4,2,3,2,128,128]{6,5,4,3,2,1,0:T(8,128)(2,1)}, u32[]{:S(2)}, u32[]{:S(2)}) collective-permute-start(bf16[4,4,2,3,2,128,128]{6,5,4,3,2,1,0:T(8,128)(2,1)} %all-gather.2.cloned.1.call-done), channel_id=1, source_target_pairs={{1,0},{2,1},{3,2},{4,3},{5,4},{6,5},{7,6},{8,7},{9,8},{10,9},{11,1... | collective-permute-start | bytes 18874376 | tf_op jit(solution)/shard_map/ppermute | solution.py:21
  405.3 133.1 %slice-start.2 = ((s8[6291456]{0:T(1024)(128)(4,1)}), s8[4194304]{0:T(1024)(128)(4,1)S(1)}, s32[]{:S(2)}) async-start(s8[6291456]{0:T(1024)(128)(4,1)} %bitcast.778), calls=%async_computation.3 | async-start | bytes 8388608
  405.3 133.1 %slice-start.3 = ((s8[6291456]{0:T(1024)(128)(4,1)}), s8[2097152]{0:T(1024)(128)(4,1)S(1)}, s32[]{:S(2)}) async-start(s8[6291456]{0:T(1024)(128)(4,1)} %bitcast.778), calls=%async_computation.4 | async-start | bytes 4194304
  692.4 19.0 %copy-start.3 = (f32[4,4,3,2,128,128]{5,4,3,2,1,0:T(8,128)S(1)}, f32[4,4,3,2,128,128]{5,4,3,2,1,0:T(8,128)}, u32[]{:S(2)}) copy-start(f32[4,4,3,2,128,128]{5,4,3,2,1,0:T(8,128)} %get-tuple-element.15) | copy-start | bytes 18874372
  711.4 27.5 %slice-start = ((s8[6291456]{0:T(1024)(128)(4,1)}), s8[4194304]{0:T(1024)(128)(4,1)S(1)}, s32[]{:S(2)}) async-start(s8[6291456]{0:T(1024)(128)(4,1)} %bitcast.775), calls=%async_computation.1 | async-start | bytes 8388608
  725.2 13.6 %slice-start.1 = ((s8[6291456]{0:T(1024)(128)(4,1)}), s8[2097152]{0:T(1024)(128)(4,1)S(1)}, s32[]{:S(2)}) async-start(s8[6291456]{0:T(1024)(128)(4,1)} %bitcast.775), calls=%async_computation.2 | async-start | bytes 4194304
  738.8 15.8 %copy-start.1 = (f32[3,128,128]{2,1,0:T(8,128)S(1)}, f32[3,128,128]{2,1,0:T(8,128)}, u32[]{:S(2)}) copy-start(f32[3,128,128]{2,1,0:T(8,128)} %param.13) | copy-start | bytes 589828
Sparse Core Ops, SparseCore 0:
  340.3 50.9 all-gather.1

commit v2 on v1

--- a/solution.py
+++ b/solution.py
@@ -201,15 +201,27 @@
         great_term = (occupied + 1.0) * lower_side[:, :, 1].astype(
             jnp.float32
         ) + occupied * upper_side[:, :, 1].astype(jnp.float32)
-        less_sum = form_factor[mode_index] * jnp.einsum(
-            "ak,kesrij->aesrij", weights[mode_index], less_term, precision=lax.Precision.HIGHEST
-        )
-        great_sum = form_factor[mode_index] * jnp.einsum(
-            "ak,kesrij->aesrij", weights[mode_index], great_term, precision=lax.Precision.HIGHEST
-        )
+        mode_weights = weights[mode_index][:, :, None, None, None, None, None]
+        less_sum = form_factor[mode_index] * jnp.sum(mode_weights * less_term[None], axis=1)
+        great_sum = form_factor[mode_index] * jnp.sum(mode_weights * great_term[None], axis=1)
         total_less = less_sum if total_less is None else total_less + less_sum
         total_great = great_sum if total_great is None else total_great + great_sum
     return (total_less, total_great)
+
+
+def exchange_blocks(blocks, width):
+    count = lax.axis_size("kz")
+    momentum = lax.axis_index("kz")
+    far_pairs = [(i, (i + 2) % count) for i in range(count)]
+    near_pairs = [(i, i ^ 1) for i in range(count)]
+    far = lax.ppermute(blocks, "kz", far_pairs)
+    local_pair = jnp.concatenate([blocks, far], axis=0)
+    extended = padded(local_pair, (("en", 1),), width)
+    other = lax.ppermute(extended, "kz", near_pairs)
+    everyone = jnp.concatenate([extended, other], axis=0)
+    partner = momentum ^ 1
+    order = jnp.stack([momentum, (momentum + 2) % count, partner, (partner + 2) % count])
+    return everyone, order
 
 
 def on_device(
@@ -237,8 +249,8 @@
     blocks = green_blocks(sigma_less, sigma_great, hamilton, slab_coupling, energies)
     table_rows = lax.dynamic_slice_in_dim(kz_table, momenta_start, momenta_local, 0)
     weights = momentum_weights(table_rows, mode_weight, momenta_total)
-    everyone = lax.all_gather(blocks, "kz", axis=0, tiled=True)
-    extended = padded(everyone, (("en", 1),), OFFMAX)
+    extended, order = exchange_blocks(blocks, OFFMAX)
+    weights = jnp.take(weights, order, axis=2)
     less_total, great_total = mixed_sums(
         extended, weights, form_factor, occupation, energy_offset, energy_local, OFFMAX
     )

time: 774 us -> 576 us (0.74)
  waiting for transfers between devices: 300 us -> 173 us
  matrix products: 168 us -> 108 us
  other arithmetic: 28.1 us -> 48.8 us
  local copies, waits for them, and re-layouts: 46.6 us -> 26.5 us
  between operations: 22.7 us -> 8.81 us
    ppermute x1, waiting for transfers between devices: 125 us -> 64.5 us  [padded(): lax.ppermute(lax.slice_in_dim(block, block.shape[dim] - width, None, axis...]
    dot_general x4 -> x0, matrix products: 60.2 us -> none  [the longest x2 32.8 us: mixed_sums(): jnp.einsum('ak,kesrij->aesrij', weights[mode_index], less_term, precision...]
    ppermute x1, waiting for transfers between devices: 124 us -> 68.4 us  [padded(): lax.ppermute(lax.slice_in_dim(block, 0, width, axis=dim), axis, backward)]
    all_gather x1 -> x0, waiting for transfers between devices: 51.1 us -> none  [on_device(): everyone = lax.all_gather(blocks, 'kz', axis=0, tiled=True)]
    ppermute x0 -> x2, waiting for transfers between devices: none -> 40.5 us  [the longest x1 35.6 us: exchange_blocks(): far = lax.ppermute(blocks, 'kz', far_pairs)]
    concatenate x0 -> x3, other arithmetic: none -> 23.1 us  [the longest x1 18.2 us: exchange_blocks(): everyone = jnp.concatenate([extended, other], axis=0)]
    add x1 -> x0, other arithmetic: 18.2 us -> none  [mixed_sums(): (occupied + 1.0) * lower_side[:, :, 1].astype(jnp.float32)]
    reduce_sum x0 -> x1, other arithmetic: none -> 14.8 us  [mixed_sums(): jnp.sum(mode_weights * great_term[None], axis=1)]
  transfers between devices with their start and end apart: 3 -> 4, of which waited for: 3 -> 4; matrix products, arithmetic and copies ran while one was open for 2% -> 1% of each run, Pallas kernels for 0% -> 0%
where the time goes in v2:
time: 576 us; the launch traced here: 566 us
  Pallas kernels  191 us (33%)
  waiting for transfers between devices  173 us (30%)
  matrix products  108 us (19%)
  other arithmetic  48.8 us (8%)
  local copies, waits for them, and re-layouts  26.5 us (5%)
  starting transfers between devices  9.21 us (2%)
  between operations  8.81 us (2%)
    pallas_call x3, Pallas kernels, hermitian_inverse(): pl.pallas_call(sweep_kernel, out_shape=(out_shape, out_shape), interpret=...  191 us
    dot_general x116, matrix products, matmul_high(): jnp.matmul(left_matrix, right_matrix, precision=lax.Precision.HIGHEST)  106 us
    ppermute x1, waiting for transfers between devices, padded(): lax.ppermute(lax.slice_in_dim(block, 0, width, axis=dim), axis, backward)  68.4 us
    ppermute x1, waiting for transfers between devices, padded(): lax.ppermute(lax.slice_in_dim(block, block.shape[dim] - width, None, axis...  64.5 us
    ppermute x1, waiting for transfers between devices, exchange_blocks(): far = lax.ppermute(blocks, 'kz', far_pairs)  35.6 us
    concatenate x1, other arithmetic, exchange_blocks(): everyone = jnp.concatenate([extended, other], axis=0)  18.2 us
    reduce_sum x1, other arithmetic, mixed_sums(): jnp.sum(mode_weights * great_term[None], axis=1)  14.8 us
  transfers between devices with their start and end apart: 4, of which 4 were waited for; matrix products, arithmetic and copies ran while one was open for 1% of the time, Pallas kernels for 0%

profile of v2, /device:TPU:63, one launch (start us, length us, event | category | flops | bytes accessed | tf_op | source)
XLA Modules:
  0.0 566.1 jit_solution(4120988152284675421)
XLA Ops:
  1.9 2.0 fusion.259
  10.5 63.7 %shard_map.122 = (f32[4,128,128]{2,1,0:T(8,128)}, f32[4,128,128]{2,1,0:T(8,128)}) custom-call(f32[4,128,128]{2,1,0:T(8,128)} %convolution_subtract_fusion.25.normal_re_ref, f32[4,128,128]{2,1,0:T(8,128)} %convolution_add_fusion.25.normal_im_ref), custom_call_target="tpu_custom_call" | custom-call | tf_op jit(solution)/shard_map/pallas_call | solution.py:98
  74.3 1.6 fusion.125
  75.9 1.7 fusion.131
  77.6 1.7 convolution_add_fusion.24
  79.3 1.6 convolution_subtract_fusion.24
  82.2 2.1 fusion.61
  89.3 63.7 %shard_map.123 = (f32[4,128,128]{2,1,0:T(8,128)}, f32[4,128,128]{2,1,0:T(8,128)}) custom-call(f32[4,128,128]{2,1,0:T(8,128)} %convolution_subtract_fusion.19.normal_re_ref, f32[4,128,128]{2,1,0:T(8,128)} %convolution_add_fusion.22.normal_im_ref), custom_call_target="tpu_custom_call" | custom-call | tf_op jit(solution)/shard_map/pallas_call | solution.py:98
  153.1 1.6 fusion.116
  154.7 1.6 fusion.37
  156.3 1.7 convolution_subtract_fusion.18
  159.0 1.6 convolution_add_fusion.20
  161.2 1.5 convolution_subtract_fusion.14
  162.7 1.5 convolution_subtract_fusion.15
  168.1 63.7 %shard_map.124 = (f32[4,128,128]{2,1,0:T(8,128)}, f32[4,128,128]{2,1,0:T(8,128)}) custom-call(f32[4,128,128]{2,1,0:T(8,128)} %convolution_subtract_fusion.13.normal_re_ref, f32[4,128,128]{2,1,0:T(8,128)} %convolution_add_fusion.16.normal_im_ref), custom_call_target="tpu_custom_call" | custom-call | tf_op jit(solution)/shard_map/pallas_call | solution.py:98
  231.8 1.7 fusion.30
  233.5 1.6 fusion.95
  239.0 1.5 convolution_add_fusion.18
  269.2 1.6 fusion.280
  273.3 1.8 copy.195
  276.9 2.0 fusion.24
  280.7 2.2 fusion.18
  282.9 1.8 copy.201
  284.8 2.0 fusion.25
  288.1 1.7 convolution_subtract_fusion.5
  296.3 1.8 convert_bitcast_fusion.1
  301.3 2.3 convolution_subtract_fusion.1
  303.6 1.8 copy.208
  305.4 2.0 fusion.10
  307.5 1.8 copy.218
  311.1 2.3 fusion.11
  313.4 1.8 copy.215
  315.2 2.1 fusion.9
  317.3 1.9 copy.219
  319.2 1.6 copy.216
  321.7 1.7 convert_bitcast_fusion.2
  327.5 2.0 convert_bitcast_fusion.5
  329.4 1.9 convert_bitcast_fusion.4
  333.4 35.6 %collective-permute-done = bf16[1,4,2,3,2,128,128]{5,6,1,4,3,2,0:T(8,128)(2,1)S(1)} collective-permute-done((bf16[1,4,2,3,2,128,128]{5,6,1,4,3,2,0:T(8,128)(2,1)S(1)}, bf16[1,4,2,3,2,128,128]{5,6,1,4,3,2,0:T(8,128)(2,1)S(1)}, u32[]{:S(2)}, u32[]{:S(2)}) %collective-permute-start) | collective-permute-done | bytes 1572896 | tf_op jit(solution)/shard_map/ppermute | solution.py:217
  369.4 3.6 collective-permute-start.1
  373.0 1.9 collective-permute-start.2
  374.9 64.5 %collective-permute-done.1 = bf16[2,4,2,3,2,128,128]{5,6,1,4,3,2,0:T(8,128)(2,1)S(1)} collective-permute-done((bf16[2,4,2,3,2,128,128]{5,6,1,4,3,2,0:T(8,128)(2,1)S(1)}, bf16[2,4,2,3,2,128,128]{5,6,1,4,3,2,0:T(8,128)(2,1)S(1)}, u32[]{:S(2)}, u32[]{:S(2)}) %collective-permute-start.1) | collective-permute-done | bytes 3145760 | tf_op jit(solution)/shard_map/ppermute | solution.py:18
  439.5 68.4 %collective-permute-done.2 = bf16[2,4,2,3,2,128,128]{5,6,1,4,3,2,0:T(8,128)(2,1)S(1)} collective-permute-done((bf16[2,4,2,3,2,128,128]{5,6,1,4,3,2,0:T(8,128)(2,1)S(1)}, bf16[2,4,2,3,2,128,128]{5,6,1,4,3,2,0:T(8,128)(2,1)S(1)}, u32[]{:S(2)}, u32[]{:S(2)}) %collective-permute-start.2) | collective-permute-done | bytes 3145760 | tf_op jit(solution)/shard_map/ppermute | solution.py:21
  507.9 4.6 pad_maximum_fusion.1
  512.5 2.5 collective-permute-start.3
  524.7 4.9 collective-permute-done.3
  529.6 18.2 %pad_maximum_fusion = bf16[4,12,2,3,2,128,128]{5,6,1,4,3,2,0:T(8,128)(2,1)} fusion(bf16[2,12,2,3,2,128,128]{5,6,1,4,3,2,0:T(8,128)(2,1)} %collective-permute-done.3, bf16[2,4,2,3,2,128,128]{5,6,1,4,3,2,0:T(8,128)(2,1)} %copy-done.4, bf16[1,4,2,3,2,128,128]{5,6,1,4,3,2,0:T(8,128)(2,1)S(1)} %collective-permute-done, ...), kind=kLoop, calls=%fused_computation.1 | loop fusion | flops 47185920 | bytes 37748736 | tf_op jit(solution)/shard_map/concatenate | solution.py:221
  547.8 14.8 %fusion.1 = (f32[4,3,2,128,128]{3,4,0,2,1:T(8,128)S(1)}, f32[4,3,2,128,128]{3,4,0,2,1:T(8,128)S(1)}, f32[4,3,2,128,128]{3,4,0,2,1:T(8,128)S(1)}, f32[4,3,2,128,128]{3,4,0,2,1:T(8,128)S(1)}) fusion(bf16[4,12,2,3,2,128,128]{5,6,1,4,3,2,0:T(8,128)(2,1)} %pad_maximum_fusion, s32[]{:T(128)S(6)} %select_n.60, s32[]{:T(128)S(6)} %add.472, s32[]{:T(128)S(6)} %select_n.61, ...), kind=kLoop, calls=%fused_computation.8 | loop fusion | flops 42467328 | bytes 31457348 | tf_op jit(solution)/shard_map/reduce_sum | solution.py:206
  (208 shorter events, 83.9 us)
Async XLA Ops:
  0.6 3.4 copy-start
  5.6 75.3 %copy-start.2 = (f32[2,128,128]{2,1,0:T(8,128)S(1)}, f32[2,128,128]{2,1,0:T(8,128)}, u32[]{:S(2)}) copy-start(f32[2,128,128]{2,1,0:T(8,128)} %param.15) | copy-start | bytes 393220
  82.2 74.1 %copy-start.14 = (f32[1,4,2,128,128]{4,3,1,2,0:T(8,128)}, f32[1,4,2,128,128]{4,3,1,2,0:T(8,128)S(1)}, u32[]{:S(2)}) copy-start(f32[1,4,2,128,128]{4,3,1,2,0:T(8,128)S(1)} %get-tuple-element.56) | copy-start | bytes 1572868
  156.3 79.2 %copy-start.21 = (bf16[1,4,2,128,128]{4,3,1,2,0:T(8,128)(2,1)S(1)}, bf16[1,4,2,128,128]{4,3,1,2,0:T(8,128)(2,1)}, u32[]{:S(2)}) copy-start(bf16[1,4,2,128,128]{4,3,1,2,0:T(8,128)(2,1)} %get-tuple-element.40) | copy-start | bytes 786436
  231.8 10.2 %copy-start.15 = (f32[1,4,2,128,128]{4,3,1,2,0:T(8,128)S(1)}, f32[1,4,2,128,128]{4,3,1,2,0:T(8,128)}, u32[]{:S(2)}) copy-start(f32[1,4,2,128,128]{4,3,1,2,0:T(8,128)} %copy-done.14) | copy-start | bytes 1572868
  235.5 29.8 %copy-start.10 = (f32[4,128,128]{2,1,0:T(8,128)}, f32[4,128,128]{2,1,0:T(8,128)S(1)}, u32[]{:S(2)}) copy-start(f32[4,128,128]{2,1,0:T(8,128)S(1)} %fusion.189) | copy-start | bytes 786436
  236.0 8.7 %copy-start.24 = (f32[4,128,128]{2,1,0:T(8,128)S(1)}, f32[4,128,128]{2,1,0:T(8,128)}, u32[]{:S(2)}) copy-start(f32[4,128,128]{2,1,0:T(8,128)} %get-tuple-element.13) | copy-start | bytes 786436
  248.0 9.1 %copy-start.8 = (f32[4,128,128]{2,1,0:T(8,128)}, f32[4,128,128]{2,1,0:T(8,128)S(1)}, u32[]{:S(2)}) copy-start(f32[4,128,128]{2,1,0:T(8,128)S(1)} %convolution_subtract_fusion.16) | copy-start | bytes 786436
  248.7 23.2 %copy-start.7 = (f32[4,128,128]{1,2,0:T(8,128)}, f32[4,128,128]{1,2,0:T(8,128)S(1)}, u32[]{:S(2)}) copy-start(f32[4,128,128]{1,2,0:T(8,128)S(1)} %convolution_add_fusion.13) | copy-start | bytes 786436
  257.8 4.9 copy-start.18
  264.4 8.8 %copy-start.11 = (f32[4,128,128]{2,1,0:T(8,128)}, f32[4,128,128]{2,1,0:T(8,128)S(1)}, u32[]{:S(2)}) copy-start(f32[4,128,128]{2,1,0:T(8,128)S(1)} %fusion.209) | copy-start | bytes 786436
  266.1 7.2 %copy-start.9 = (f32[4,128,128]{2,1,0:T(8,128)}, f32[4,128,128]{2,1,0:T(8,128)S(1)}, u32[]{:S(2)}) copy-start(f32[4,128,128]{2,1,0:T(8,128)S(1)} %fusion.181) | copy-start | bytes 786436
  266.9 1.5 copy-start.5
  276.9 3.8 copy-start.23
  278.9 0.7 copy-start.16
  279.6 20.0 %copy-start.12 = (f32[4,128,128]{2,1,0:T(8,128)S(1)}, f32[4,128,128]{2,1,0:T(8,128)}, u32[]{:S(2)}) copy-start(f32[4,128,128]{2,1,0:T(8,128)} %copy-done.11) | copy-start | bytes 786436
  284.7 10.7 %copy-start.17 = (f32[1,4,128,128]{3,2,1,0:T(8,128)S(1)}, f32[1,4,128,128]{3,2,1,0:T(8,128)}, u32[]{:S(2)}) copy-start(f32[1,4,128,128]{3,2,1,0:T(8,128)} %copy-done.16) | copy-start | bytes 786436
  286.7 9.5 %copy-start.19 = (f32[1,4,128,128]{2,3,1,0:T(8,128)}, f32[1,4,128,128]{2,3,1,0:T(8,128)S(1)}, u32[]{:S(2)}) copy-start(f32[1,4,128,128]{2,3,1,0:T(8,128)S(1)} %fusion.25) | copy-start | bytes 786436
  288.1 21.2 %copy-start.13 = (f32[4,128,128]{2,1,0:T(8,128)S(1)}, f32[4,128,128]{2,1,0:T(8,128)}, u32[]{:S(2)}) copy-start(f32[4,128,128]{2,1,0:T(8,128)} %copy-done.11) | copy-start | bytes 786436
  296.3 24.6 %copy-start.6 = (f32[4,128,128]{2,1,0:T(8,128)S(1)}, f32[4,128,128]{2,1,0:T(8,128)}, u32[]{:S(2)}) copy-start(f32[4,128,128]{2,1,0:T(8,128)} %copy-done.5) | copy-start | bytes 786436
  298.1 23.6 %copy-start.20 = (f32[1,4,128,128]{2,3,1,0:T(8,128)S(1)}, f32[1,4,128,128]{2,3,1,0:T(8,128)}, u32[]{:S(2)}) copy-start(f32[1,4,128,128]{2,3,1,0:T(8,128)} %copy-done.19) | copy-start | bytes 786436
  315.2 16.2 %copy-start.25 = (bf16[1,4,1,128,128]{3,4,1,2,0:T(8,128)(2,1)S(1)}, bf16[1,4,1,128,128]{3,4,1,2,0:T(8,128)(2,1)}, u32[]{:S(2)}) copy-start(bf16[1,4,1,128,128]{3,4,1,2,0:T(8,128)(2,1)} %convert_bitcast_fusion) | copy-start | bytes 393220
  317.3 12.1 %copy-start.22 = (f32[1,4,128,128]{3,2,1,0:T(8,128)S(1)}, f32[1,4,128,128]{3,2,1,0:T(8,128)}, u32[]{:S(2)}) copy-start(f32[1,4,128,128]{3,2,1,0:T(8,128)} %fusion.9) | copy-start | bytes 786436
  323.3 8.0 %copy-start.26 = (bf16[1,4,1,128,128]{3,4,1,2,0:T(8,128)(2,1)S(1)}, bf16[1,4,1,128,128]{3,4,1,2,0:T(8,128)(2,1)}, u32[]{:S(2)}) copy-start(bf16[1,4,1,128,128]{3,4,1,2,0:T(8,128)(2,1)} %copy.216) | copy-start | bytes 393220
  324.1 7.3 %copy-start.27 = (bf16[1,4,1,128,128]{3,4,1,2,0:T(8,128)(2,1)S(1)}, bf16[1,4,1,128,128]{3,4,1,2,0:T(8,128)(2,1)}, u32[]{:S(2)}) copy-start(bf16[1,4,1,128,128]{3,4,1,2,0:T(8,128)(2,1)} %copy.217) | copy-start | bytes 393220
  326.4 5.0 copy-start.29
  326.4 5.1 copy-start.28
  332.2 36.8 %collective-permute-start = (bf16[1,4,2,3,2,128,128]{5,6,1,4,3,2,0:T(8,128)(2,1)S(1)}, bf16[1,4,2,3,2,128,128]{5,6,1,4,3,2,0:T(8,128)(2,1)S(1)}, u32[]{:S(2)}, u32[]{:S(2)}) collective-permute-start(bf16[1,4,2,3,2,128,128]{5,6,1,4,3,2,0:T(8,128)(2,1)S(1)} %pad_maximum_fusion.3), channel_id=1, source_target_pairs={{0,64},{32,96},{64,0},{96,32},{1,65},{33,97},{65,1},{97,33},{2,66}... | collective-permute-start | bytes 4718600 | tf_op jit(solution)/shard_map/ppermute | solution.py:217
  369.4 145.6 %copy-start.31 = (s32[2]{0:T(128)S(1)}, s32[2]{0:T(128)}, u32[]{:S(2)}) copy-start(s32[2]{0:T(128)} %param.21) | copy-start | bytes 28
  369.4 152.0 %copy-start.33 = (f32[2,4]{1,0:T(2,128)S(1)}, f32[2,4]{1,0:T(2,128)}, u32[]{:S(2)}) copy-start(f32[2,4]{1,0:T(2,128)} %param.18) | copy-start | bytes 100
  369.4 153.1 %copy-start.32 = (f32[2]{0:T(128)S(1)}, f32[2]{0:T(128)}, u32[]{:S(2)}) copy-start(f32[2]{0:T(128)} %param.20) | copy-start | bytes 28
  369.4 154.9 %copy-start.30 = (f32[2,128,128]{2,1,0:T(8,128)S(1)}, f32[2,128,128]{2,1,0:T(8,128)}, u32[]{:S(2)}) copy-start(f32[2,128,128]{2,1,0:T(8,128)} %param.19) | copy-start | bytes 393220
  369.4 70.1 %collective-permute-start.1 = (bf16[2,4,2,3,2,128,128]{5,6,1,4,3,2,0:T(8,128)(2,1)S(1)}, bf16[2,4,2,3,2,128,128]{5,6,1,4,3,2,0:T(8,128)(2,1)S(1)}, u32[]{:S(2)}, u32[]{:S(2)}) collective-permute-start(bf16[2,4,2,3,2,128,128]{5,6,1,4,3,2,0:T(8,128)(2,1)S(1)} %pad_maximum_fusion.2), channel_id=1, source_target_pairs={{0,1},{1,2},{2,3},{3,4},{4,5},{5,6},{6,7},{7,8},{8,9},{9,10},{10,1... | collective-permute-start | bytes 9437192 | tf_op jit(solution)/shard_map/ppermute | solution.py:18
  373.0 134.9 %collective-permute-start.2 = (bf16[2,4,2,3,2,128,128]{5,6,1,4,3,2,0:T(8,128)(2,1)S(1)}, bf16[2,4,2,3,2,128,128]{5,6,1,4,3,2,0:T(8,128)(2,1)S(1)}, u32[]{:S(2)}, u32[]{:S(2)}) collective-permute-start(bf16[2,4,2,3,2,128,128]{5,6,1,4,3,2,0:T(8,128)(2,1)S(1)} %pad_maximum_fusion.2), channel_id=1, source_target_pairs={{1,0},{2,1},{3,2},{4,3},{5,4},{6,5},{7,6},{8,7},{9,8},{10,9},{11,1... | collective-permute-start | bytes 9437192 | tf_op jit(solution)/shard_map/ppermute | solution.py:21
  439.5 73.0 %copy-start.3 = (bf16[2,4,2,3,2,128,128]{5,6,1,4,3,2,0:T(8,128)(2,1)}, bf16[2,4,2,3,2,128,128]{5,6,1,4,3,2,0:T(8,128)(2,1)S(1)}, u32[]{:S(2)}) copy-start(bf16[2,4,2,3,2,128,128]{5,6,1,4,3,2,0:T(8,128)(2,1)S(1)} %collective-permute-done.1) | copy-start | bytes 9437188
  507.9 4.6 copy-start.4
  512.5 17.1 %collective-permute-start.3 = (bf16[2,12,2,3,2,128,128]{5,6,1,4,3,2,0:T(8,128)(2,1)}, bf16[2,12,2,3,2,128,128]{5,6,1,4,3,2,0:T(8,128)(2,1)}, u32[]{:S(2)}, u32[]{:S(2)}) collective-permute-start(bf16[2,12,2,3,2,128,128]{5,6,1,4,3,2,0:T(8,128)(2,1)} %pad_maximum_fusion.1), channel_id=1, source_target_pairs={{0,32},{32,0},{64,96},{96,64},{1,33},{33,1},{65,97},{97,65},{2,34}... | collective-permute-start | bytes 28311560 | tf_op jit(solution)/shard_map/ppermute | solution.py:220
  547.8 17.8 %copy-start.1 = (f32[3,128,128]{2,1,0:T(8,128)S(1)}, f32[3,128,128]{2,1,0:T(8,128)}, u32[]{:S(2)}) copy-start(f32[3,128,128]{2,1,0:T(8,128)} %param.13) | copy-start | bytes 589828

commit v3 on v2

--- a/solution.py
+++ b/solution.py
@@ -161,9 +161,10 @@
         full_ret = add_pair(left_ret[slab_index], complex_product(bridge, left_ret[slab_index]))
         lesser_list.insert(0, full_less)
         greater_list.insert(0, greater_of(full_less, full_ret))
-    lesser_all = jnp.stack([pack_pair(item) for item in lesser_list], axis=2)
-    greater_all = jnp.stack([pack_pair(item) for item in greater_list], axis=2)
-    return jnp.stack([lesser_all, greater_all], axis=2).astype(jnp.bfloat16)
+    return [
+        jnp.stack([pack_pair(less_item), pack_pair(great_item)], axis=2).astype(jnp.bfloat16)
+        for less_item, great_item in zip(lesser_list, greater_list)
+    ]
 
 
 def hamiltonian(onsite_table, cos_coupling, slab_kind, momenta_index, momenta_total):
@@ -201,7 +202,9 @@
         great_term = (occupied + 1.0) * lower_side[:, :, 1].astype(
             jnp.float32
         ) + occupied * upper_side[:, :, 1].astype(jnp.float32)
-        mode_weights = weights[mode_index][:, :, None, None, None, None, None]
+        mode_weights = weights[mode_index].reshape(
+            weights.shape[1:] + (1,) * (less_term.ndim - 1)
+        )
         less_sum = form_factor[mode_index] * jnp.sum(mode_weights * less_term[None], axis=1)
         great_sum = form_factor[mode_index] * jnp.sum(mode_weights * great_term[None], axis=1)
         total_less = less_sum if total_less is None else total_less + less_sum
@@ -215,8 +218,9 @@
     far_pairs = [(i, (i + 2) % count) for i in range(count)]
     near_pairs = [(i, i ^ 1) for i in range(count)]
     far = lax.ppermute(blocks, "kz", far_pairs)
-    local_pair = jnp.concatenate([blocks, far], axis=0)
-    extended = padded(local_pair, (("en", 1),), width)
+    own_extended = padded(blocks, (("en", 1),), width)
+    far_extended = padded(far, (("en", 1),), width)
+    extended = jnp.concatenate([own_extended, far_extended], axis=0)
     other = lax.ppermute(extended, "kz", near_pairs)
     everyone = jnp.concatenate([extended, other], axis=0)
     partner = momentum ^ 1
@@ -246,15 +250,25 @@
     energy_index = lax.axis_index("en") * energy_local + jnp.arange(energy_local, dtype=jnp.int32)
     energies = -1.5 + 3.0 * (energy_index.astype(jnp.float32) + 0.5) / energy_total
     hamilton = hamiltonian(onsite_table, cos_coupling, slab_kind, momenta_index, momenta_total)
-    blocks = green_blocks(sigma_less, sigma_great, hamilton, slab_coupling, energies)
+    slab_blocks = green_blocks(sigma_less, sigma_great, hamilton, slab_coupling, energies)
     table_rows = lax.dynamic_slice_in_dim(kz_table, momenta_start, momenta_local, 0)
     weights = momentum_weights(table_rows, mode_weight, momenta_total)
-    extended, order = exchange_blocks(blocks, OFFMAX)
-    weights = jnp.take(weights, order, axis=2)
-    less_total, great_total = mixed_sums(
-        extended, weights, form_factor, occupation, energy_offset, energy_local, OFFMAX
-    )
-    return (less_total.astype(jnp.bfloat16), great_total.astype(jnp.bfloat16))
+    less_parts = []
+    great_parts = []
+    for blocks in slab_blocks:
+        extended, order = exchange_blocks(blocks, OFFMAX)
+        less_part, great_part = mixed_sums(
+            extended,
+            jnp.take(weights, order, axis=2),
+            form_factor,
+            occupation,
+            energy_offset,
+            energy_local,
+            OFFMAX,
+        )
+        less_parts.append(less_part.astype(jnp.bfloat16))
+        great_parts.append(great_part.astype(jnp.bfloat16))
+    return (jnp.stack(less_parts, axis=2), jnp.stack(great_parts, axis=2))
 
 
 def solution(mesh):

time: 576 us -> 515 us (0.89)
  waiting for transfers between devices: 173 us -> 81.7 us
  starting transfers between devices: 9.21 us -> 55.6 us
  matrix products: 108 us -> 98.3 us
    ppermute x1 -> x6, waiting for transfers between devices: 64.5 us -> 28.3 us  [padded(): lax.ppermute(lax.slice_in_dim(block, block.shape[dim] - width, None, axis...]
    ppermute x1 -> x3, waiting for transfers between devices: 35.6 us -> 0.01 us  [exchange_blocks(): far = lax.ppermute(blocks, 'kz', far_pairs)]
    ppermute x1 -> x6, starting transfers between devices: 3.6 us -> 23.2 us  [padded(): lax.ppermute(lax.slice_in_dim(block, block.shape[dim] - width, None, axis...]
    ppermute x1 -> x6, waiting for transfers between devices: 68.4 us -> 53.4 us  [padded(): lax.ppermute(lax.slice_in_dim(block, 0, width, axis=dim), axis, backward)]
    ppermute x1 -> x6, starting transfers between devices: 1.92 us -> 15.2 us  [padded(): lax.ppermute(lax.slice_in_dim(block, 0, width, axis=dim), axis, backward)]
    ppermute x1 -> x3, starting transfers between devices: 2.48 us -> 12.5 us  [exchange_blocks(): other = lax.ppermute(extended, 'kz', near_pairs)]
    dot_general x116, matrix products: 106 us -> 97.6 us  [matmul_high(): jnp.matmul(left_matrix, right_matrix, precision=lax.Precision.HIGHEST)]
    concatenate x1 -> x3, other arithmetic: 18.2 us -> 13.6 us  [exchange_blocks(): everyone = jnp.concatenate([extended, other], axis=0)]
  transfers between devices with their start and end apart: 4 -> 18, of which waited for: 4 -> 5; matrix products, arithmetic and copies ran while one was open for 1% -> 11% of each run, Pallas kernels for 0% -> 0%
where the time goes in v3:
time: 515 us; the launch traced here: 505 us
  Pallas kernels  191 us (37%)
  matrix products  98.3 us (19%)
  waiting for transfers between devices  81.7 us (16%)
  starting transfers between devices  55.6 us (11%)
  other arithmetic  44.2 us (9%)
  local copies, waits for them, and re-layouts  24.9 us (5%)
  between operations  9.31 us (2%)
    pallas_call x3, Pallas kernels, hermitian_inverse(): pl.pallas_call(sweep_kernel, out_shape=(out_shape, out_shape), interpret=...  191 us
    dot_general x116, matrix products, matmul_high(): jnp.matmul(left_matrix, right_matrix, precision=lax.Precision.HIGHEST)  97.6 us
    ppermute x6, waiting for transfers between devices, padded(): lax.ppermute(lax.slice_in_dim(block, 0, width, axis=dim), axis, backward)  53.4 us
    ppermute x6, waiting for transfers between devices, padded(): lax.ppermute(lax.slice_in_dim(block, block.shape[dim] - width, None, axis...  28.3 us
    ppermute x6, starting transfers between devices, padded(): lax.ppermute(lax.slice_in_dim(block, block.shape[dim] - width, None, axis...  23.2 us
    ppermute x6, starting transfers between devices, padded(): lax.ppermute(lax.slice_in_dim(block, 0, width, axis=dim), axis, backward)  15.2 us
    concatenate x3, other arithmetic, exchange_blocks(): everyone = jnp.concatenate([extended, other], axis=0)  13.6 us
    ppermute x3, starting transfers between devices, exchange_blocks(): other = lax.ppermute(extended, 'kz', near_pairs)  12.5 us
  transfers between devices with their start and end apart: 18, of which 5 were waited for; matrix products, arithmetic and copies ran while one was open for 11% of the time, Pallas kernels for 0%

profile of v3, /device:TPU:63, one launch (start us, length us, event | category | flops | bytes accessed | tf_op | source)
XLA Modules:
  0.0 505.3 jit_solution(8622165019334239872)
XLA Ops:
  8.6 63.8 %shard_map.122 = (f32[4,128,128]{2,1,0:T(8,128)}, f32[4,128,128]{2,1,0:T(8,128)}) custom-call(f32[4,128,128]{2,1,0:T(8,128)} %convolution_subtract_fusion.25.normal_re_ref, f32[4,128,128]{2,1,0:T(8,128)} %convolution_add_fusion.25.normal_im_ref), custom_call_target="tpu_custom_call" | custom-call | tf_op jit(solution)/shard_map/pallas_call | solution.py:98
  72.4 1.7 fusion.141
  74.1 1.7 fusion.147
  75.7 1.7 convolution_add_fusion.24
  85.5 63.7 %shard_map.123 = (f32[4,128,128]{2,1,0:T(8,128)}, f32[4,128,128]{2,1,0:T(8,128)}) custom-call(f32[4,128,128]{2,1,0:T(8,128)} %convolution_subtract_fusion.19.normal_re_ref, f32[4,128,128]{2,1,0:T(8,128)} %convolution_add_fusion.22.normal_im_ref), custom_call_target="tpu_custom_call" | custom-call | tf_op jit(solution)/shard_map/pallas_call | solution.py:98
  149.3 1.7 fusion.132
  150.9 1.6 fusion.53
  152.6 1.7 convolution_subtract_fusion.18
  161.5 63.7 %shard_map.124 = (f32[4,128,128]{2,1,0:T(8,128)}, f32[4,128,128]{2,1,0:T(8,128)}) custom-call(f32[4,128,128]{2,1,0:T(8,128)} %convolution_subtract_fusion.13.normal_re_ref, f32[4,128,128]{2,1,0:T(8,128)} %convolution_add_fusion.16.normal_im_ref), custom_call_target="tpu_custom_call" | custom-call | tf_op jit(solution)/shard_map/pallas_call | solution.py:98
  226.9 1.6 fusion.111
  260.4 1.8 copy.195
  264.7 1.6 fusion.19
  267.2 2.7 fusion.22
  269.9 1.8 copy.199
  271.7 1.8 fusion.18
  273.5 2.0 fusion.28
  281.3 2.5 collective-permute-start.6
  283.9 2.7 collective-permute-start.7
  305.9 1.6 fusion.15
  311.3 1.9 convert_bitcast_fusion.5
  313.2 1.7 convert_bitcast_fusion.4
  315.9 2.6 collective-permute-start.2
  318.9 5.8 %collective-permute-start.9 = (bf16[1,4,2,2,128,128]{4,5,1,3,0,2:T(8,128)(2,1)}, bf16[1,4,2,2,128,128]{4,5,1,3,0,2:T(8,128)(2,1)S(1)}, u32[]{:S(2)}, u32[]{:S(2)}) collective-permute-start(bf16[1,4,2,2,128,128]{4,5,1,3,0,2:T(8,128)(2,1)} %collective-permute-done.8), channel_id=1, source_target_pairs={{0,1},{1,2},{2,3},{3,4},{4,5},{5,6},{6,7},{7,8},{8,9},{9,10},{10,1... | collective-permute-start | bytes 1572872 | tf_op jit(solution)/shard_map/ppermute | solution.py:18
  324.7 1.9 collective-permute-start.10
  327.9 13.2 %collective-permute-done.9 = bf16[1,4,2,2,128,128]{4,5,1,3,0,2:T(8,128)(2,1)S(1)} collective-permute-done((bf16[1,4,2,2,128,128]{4,5,1,3,0,2:T(8,128)(2,1)}, bf16[1,4,2,2,128,128]{4,5,1,3,0,2:T(8,128)(2,1)S(1)}, u32[]{:S(2)}, u32[]{:S(2)}) %collective-permute-start.9) | collective-permute-done | bytes 524320 | tf_op jit(solution)/shard_map/ppermute | solution.py:18
  343.2 5.2 %collective-permute-start = (bf16[1,4,2,2,128,128]{4,5,1,3,2,0:T(8,128)(2,1)}, bf16[1,4,2,2,128,128]{4,5,1,3,2,0:T(8,128)(2,1)S(1)}, u32[]{:S(2)}, u32[]{:S(2)}) collective-permute-start(bf16[1,4,2,2,128,128]{4,5,1,3,2,0:T(8,128)(2,1)} %pad_maximum_fusion.8), channel_id=1, source_target_pairs={{0,1},{1,2},{2,3},{3,4},{4,5},{5,6},{6,7},{7,8},{8,9},{9,10},{10,1... | collective-permute-start | bytes 1572872 | tf_op jit(solution)/shard_map/ppermute | solution.py:18
  348.4 7.1 %collective-permute-done.10 = bf16[1,4,2,2,128,128]{4,5,1,3,0,2:T(8,128)(2,1)S(1)} collective-permute-done((bf16[1,4,2,2,128,128]{4,5,1,3,0,2:T(8,128)(2,1)}, bf16[1,4,2,2,128,128]{4,5,1,3,0,2:T(8,128)(2,1)S(1)}, u32[]{:S(2)}, u32[]{:S(2)}) %collective-permute-start.10) | collective-permute-done | bytes 524320 | tf_op jit(solution)/shard_map/ppermute | solution.py:21
  355.5 1.9 collective-permute-start.3
  357.5 3.4 collective-permute-start.1
  360.9 1.9 collective-permute-start.4
  362.8 3.0 pad_maximum_fusion.4
  365.8 5.1 %collective-permute-start.11 = (bf16[2,12,2,2,128,128]{4,5,1,3,0,2:T(8,128)(2,1)}, bf16[2,12,2,2,128,128]{4,5,1,3,0,2:T(8,128)(2,1)}, u32[]{:S(2)}, u32[]{:S(2)}) collective-permute-start(bf16[2,12,2,2,128,128]{4,5,1,3,0,2:T(8,128)(2,1)} %pad_maximum_fusion.4), channel_id=1, source_target_pairs={{0,32},{32,0},{64,96},{96,64},{1,33},{33,1},{65,97},{97,65},{2,34}... | collective-permute-start | bytes 9437192 | tf_op jit(solution)/shard_map/ppermute | solution.py:224
  370.9 15.2 %collective-permute-done.3 = bf16[1,4,2,2,128,128]{4,5,1,3,2,0:T(8,128)(2,1)S(1)} collective-permute-done((bf16[1,4,2,2,128,128]{4,5,1,3,2,0:T(8,128)(2,1)}, bf16[1,4,2,2,128,128]{4,5,1,3,2,0:T(8,128)(2,1)S(1)}, u32[]{:S(2)}, u32[]{:S(2)}) %collective-permute-start.3) | collective-permute-done | bytes 524320 | tf_op jit(solution)/shard_map/ppermute | solution.py:18
  386.0 5.9 %collective-permute-start.15 = (bf16[1,4,2,2,128,128]{4,5,1,3,0,2:T(8,128)(2,1)}, bf16[1,4,2,2,128,128]{4,5,1,3,0,2:T(8,128)(2,1)S(1)}, u32[]{:S(2)}, u32[]{:S(2)}) collective-permute-start(bf16[1,4,2,2,128,128]{4,5,1,3,0,2:T(8,128)(2,1)} %collective-permute-done.14), channel_id=1, source_target_pairs={{0,1},{1,2},{2,3},{3,4},{4,5},{5,6},{6,7},{7,8},{8,9},{9,10},{10,1... | collective-permute-start | bytes 1572872 | tf_op jit(solution)/shard_map/ppermute | solution.py:18
  393.1 18.5 %collective-permute-done.4 = bf16[1,4,2,2,128,128]{4,5,1,3,2,0:T(8,128)(2,1)S(1)} collective-permute-done((bf16[1,4,2,2,128,128]{4,5,1,3,2,0:T(8,128)(2,1)}, bf16[1,4,2,2,128,128]{4,5,1,3,2,0:T(8,128)(2,1)S(1)}, u32[]{:S(2)}, u32[]{:S(2)}) %collective-permute-start.4) | collective-permute-done | bytes 524320 | tf_op jit(solution)/shard_map/ppermute | solution.py:21
  411.6 1.9 collective-permute-start.12
  413.7 3.4 collective-permute-start.13
  417.1 1.9 collective-permute-start.16
  419.0 1.8 pad_maximum_fusion.3
  421.6 5.0 collective-permute-start.5
  428.9 27.8 %collective-permute-done.16 = bf16[1,4,2,2,128,128]{4,5,1,3,0,2:T(8,128)(2,1)} collective-permute-done((bf16[1,4,2,2,128,128]{4,5,1,3,0,2:T(8,128)(2,1)}, bf16[1,4,2,2,128,128]{4,5,1,3,0,2:T(8,128)(2,1)}, u32[]{:S(2)}, u32[]{:S(2)}) %collective-permute-start.16) | collective-permute-done | bytes 524320 | tf_op jit(solution)/shard_map/ppermute | solution.py:21
  457.9 3.6 pad_maximum_fusion.5
  461.5 2.4 collective-permute-start.17
  473.6 3.8 pad_maximum_fusion.1
  477.5 3.6 pad_maximum_fusion
  481.2 6.2 %pad_maximum_fusion.2 = bf16[4,12,2,2,128,128]{4,5,1,3,0,2:T(8,128)(2,1)} fusion(bf16[2,12,2,2,128,128]{4,5,1,3,0,2:T(8,128)(2,1)} %collective-permute-done.17, bf16[1,12,2,2,128,128]{4,5,1,3,0,2:T(8,128)(2,1)S(1)} %copy-done.4, bf16[1,4,2,2,128,128]{4,5,1,3,0,2:T(8,128)(2,1)} %collective-permute-done.13, bf16[1,4,1,2,128,128]{4,5,1,3,0,2:T(8,128)(2,1)S(1)} %copy-done.26, ...), kind=kLoop, calls=%fused_computation.3 | loop fusion | flops 15728640 | bytes 12582912 | tf_op jit(solution)/shard_map/concatenate | solution.py:225
  487.4 12.3 %fusion.1 = (f32[4,2,128,128]{2,3,0,1:T(8,128)S(1)}, f32[4,2,128,128]{2,3,0,1:T(8,128)S(1)}, f32[4,2,128,128]{2,3,0,1:T(8,128)S(1)}, f32[4,2,128,128]{2,3,0,1:T(...) fusion(bf16[4,12,2,2,128,128]{4,5,1,3,0,2:T(8,128)(2,1)} %pad_m, ...), kind=kLoop, calls=%fused_computation.10 | loop fusion | flops 42467328 | bytes 31457348 | tf_op jit(solution)/shard_map/reduce_sum | solution.py:209
  499.7 2.9 fusion.38
  (309 shorter events, 103.9 us)
Async XLA Ops:
  72.4 5.0 copy-start.49
  72.4 5.7 %copy-start.2 = (f32[2,128,128]{2,1,0:T(8,128)S(1)}, f32[2,128,128]{2,1,0:T(8,128)}, u32[]{:S(2)}) copy-start(f32[2,128,128]{2,1,0:T(8,128)} %param.17) | copy-start | bytes 393220
  79.5 77.6 %copy-start.11 = (f32[1,4,2,128,128]{4,3,1,2,0:T(8,128)}, f32[1,4,2,128,128]{4,3,1,2,0:T(8,128)S(1)}, u32[]{:S(2)}) copy-start(f32[1,4,2,128,128]{4,3,1,2,0:T(8,128)S(1)} %get-tuple-element.82) | copy-start | bytes 1572868
  149.3 5.9 %copy-start.54 = (f32[4,128,128]{2,1,0:T(8,128)S(1)}, f32[4,128,128]{2,1,0:T(8,128)}, u32[]{:S(2)}) copy-start(f32[4,128,128]{2,1,0:T(8,128)} %get-tuple-element.12) | copy-start | bytes 786436
  152.5 3.9 copy-start.42
  160.2 68.6 %copy-start.33 = (bf16[1,4,2,128,128]{4,3,1,2,0:T(8,128)(2,1)S(1)}, bf16[1,4,2,128,128]{4,3,1,2,0:T(8,128)(2,1)}, u32[]{:S(2)}) copy-start(bf16[1,4,2,128,128]{4,3,1,2,0:T(8,128)(2,1)} %get-tuple-element.63) | copy-start | bytes 786436
  228.8 29.1 %copy-start.10 = (f32[4,128,128]{2,1,0:T(8,128)}, f32[4,128,128]{2,1,0:T(8,128)S(1)}, u32[]{:S(2)}) copy-start(f32[4,128,128]{2,1,0:T(8,128)S(1)} %fusion.205) | copy-start | bytes 786436
  240.8 6.5 %copy-start.5 = (f32[4,128,128]{2,1,0:T(8,128)}, f32[4,128,128]{2,1,0:T(8,128)S(1)}, u32[]{:S(2)}) copy-start(f32[4,128,128]{2,1,0:T(8,128)S(1)} %convolution_subtract_fusion.16) | copy-start | bytes 786436
  259.0 4.6 copy-start.9
  260.3 6.8 %copy-start.6 = (f32[4,128,128]{2,1,0:T(8,128)S(1)}, f32[4,128,128]{2,1,0:T(8,128)}, u32[]{:S(2)}) copy-start(f32[4,128,128]{2,1,0:T(8,128)} %copy-done.5) | copy-start | bytes 786436
  271.7 4.6 copy-start.34
  271.7 4.6 copy-start.37
  271.7 4.6 copy-start.43
  271.7 4.6 copy-start.46
  277.0 6.9 %copy-start.15 = (bf16[1,4,1,2,128,128]{4,5,1,3,0,2:T(8,128)(2,1)}, bf16[1,4,1,2,128,128]{4,5,1,3,0,2:T(8,128)(2,1)S(1)}, u32[]{:S(2)}) copy-start(bf16[1,4,1,2,128,128]{4,5,1,3,0,2:T(8,128)(2,1)S(1)} %copy.228) | copy-start | bytes 786436
  279.2 10.1 %copy-start.8 = (f32[4,128,128]{2,1,0:T(8,128)S(1)}, f32[4,128,128]{2,1,0:T(8,128)}, u32[]{:S(2)}) copy-start(f32[4,128,128]{2,1,0:T(8,128)} %copy-done.7) | copy-start | bytes 786436
  279.3 7.3 %copy-start.17 = (bf16[1,4,1,2,128,128]{4,5,1,3,0,2:T(8,128)(2,1)}, bf16[1,4,1,2,128,128]{4,5,1,3,0,2:T(8,128)(2,1)S(1)}, u32[]{:S(2)}) copy-start(bf16[1,4,1,2,128,128]{4,5,1,3,0,2:T(8,128)(2,1)S(1)} %maximum_bitcast_fusion.3) | copy-start | bytes 786436
  280.2 38.8 %collective-permute-start.8 = (bf16[1,4,2,2,128,128]{4,5,1,3,0,2:T(8,128)(2,1)}, bf16[1,4,2,2,128,128]{4,5,1,3,0,2:T(8,128)(2,1)}, u32[]{:S(2)}, u32[]{:S(2)}) collective-permute-start(bf16[1,4,2,2,128,128]{4,5,1,3,0,2:T(8,128)(2,1)} %pad_maximum_fusion.9), channel_id=1, source_target_pairs={{0,64},{32,96},{64,0},{96,32},{1,65},{33,97},{65,1},{97,33},{2,66}... | collective-permute-start | bytes 1572872 | tf_op jit(solution)/shard_map/ppermute | solution.py:220
  281.3 76.2 %collective-permute-start.6 = (bf16[1,4,2,2,128,128]{4,5,1,3,0,2:T(8,128)(2,1)}, bf16[1,4,2,2,128,128]{4,5,1,3,0,2:T(8,128)(2,1)}, u32[]{:S(2)}, u32[]{:S(2)}) collective-permute-start(bf16[1,4,2,2,128,128]{4,5,1,3,0,2:T(8,128)(2,1)} %pad_maximum_fusion.9), channel_id=1, source_target_pairs={{0,1},{1,2},{2,3},{3,4},{4,5},{5,6},{6,7},{7,8},{8,9},{9,10},{10,1... | collective-permute-start | bytes 1572872 | tf_op jit(solution)/shard_map/ppermute | solution.py:18
  283.9 77.0 %collective-permute-start.7 = (bf16[1,4,2,2,128,128]{4,5,1,3,0,2:T(8,128)(2,1)}, bf16[1,4,2,2,128,128]{4,5,1,3,0,2:T(8,128)(2,1)}, u32[]{:S(2)}, u32[]{:S(2)}) collective-permute-start(bf16[1,4,2,2,128,128]{4,5,1,3,0,2:T(8,128)(2,1)} %pad_maximum_fusion.9), channel_id=1, source_target_pairs={{1,0},{2,1},{3,2},{4,3},{5,4},{6,5},{7,6},{8,7},{9,8},{10,9},{11,1... | collective-permute-start | bytes 1572872 | tf_op jit(solution)/shard_map/ppermute | solution.py:21
  300.1 4.1 copy-start.32
  313.2 5.3 %copy-start.30 = (f32[4,128,128]{2,1,0:T(8,128)S(1)}, f32[4,128,128]{2,1,0:T(8,128)}, u32[]{:S(2)}) copy-start(f32[4,128,128]{2,1,0:T(8,128)} %copy-done.29) | copy-start | bytes 786436
  315.9 27.3 %collective-permute-start.2 = (bf16[1,4,2,2,128,128]{4,5,1,3,2,0:T(8,128)(2,1)}, bf16[1,4,2,2,128,128]{4,5,1,3,2,0:T(8,128)(2,1)}, u32[]{:S(2)}, u32[]{:S(2)}) collective-permute-start(bf16[1,4,2,2,128,128]{4,5,1,3,2,0:T(8,128)(2,1)} %pad_maximum_fusion.8), channel_id=1, source_target_pairs={{0,64},{32,96},{64,0},{96,32},{1,65},{33,97},{65,1},{97,33},{2,66}... | collective-permute-start | bytes 1572872 | tf_op jit(solution)/shard_map/ppermute | solution.py:220
  318.9 22.2 %collective-permute-start.9 = (bf16[1,4,2,2,128,128]{4,5,1,3,0,2:T(8,128)(2,1)}, bf16[1,4,2,2,128,128]{4,5,1,3,0,2:T(8,128)(2,1)S(1)}, u32[]{:S(2)}, u32[]{:S(2)}) collective-permute-start(bf16[1,4,2,2,128,128]{4,5,1,3,0,2:T(8,128)(2,1)} %collective-permute-done.8), channel_id=1, source_target_pairs={{0,1},{1,2},{2,3},{3,4},{4,5},{5,6},{6,7},{7,8},{8,9},{9,10},{10,1... | collective-permute-start | bytes 1572872 | tf_op jit(solution)/shard_map/ppermute | solution.py:18
  324.7 30.7 %collective-permute-start.10 = (bf16[1,4,2,2,128,128]{4,5,1,3,0,2:T(8,128)(2,1)}, bf16[1,4,2,2,128,128]{4,5,1,3,0,2:T(8,128)(2,1)S(1)}, u32[]{:S(2)}, u32[]{:S(2)}) collective-permute-start(bf16[1,4,2,2,128,128]{4,5,1,3,0,2:T(8,128)(2,1)} %collective-permute-done.8), channel_id=1, source_target_pairs={{1,0},{2,1},{3,2},{4,3},{5,4},{6,5},{7,6},{8,7},{9,8},{10,9},{11,1... | collective-permute-start | bytes 1572872 | tf_op jit(solution)/shard_map/ppermute | solution.py:21
  326.9 14.2 %copy-start.25 = (bf16[1,4,1,2,128,128]{4,5,1,3,0,2:T(8,128)(2,1)}, bf16[1,4,1,2,128,128]{4,5,1,3,0,2:T(8,128)(2,1)S(1)}, u32[]{:S(2)}) copy-start(bf16[1,4,1,2,128,128]{4,5,1,3,0,2:T(8,128)(2,1)S(1)} %maximum_bitcast_fusion.5) | copy-start | bytes 786436
  327.0 14.0 %copy-start.27 = (bf16[1,4,1,2,128,128]{4,5,1,3,0,2:T(8,128)(2,1)}, bf16[1,4,1,2,128,128]{4,5,1,3,0,2:T(8,128)(2,1)S(1)}, u32[]{:S(2)}) copy-start(bf16[1,4,1,2,128,128]{4,5,1,3,0,2:T(8,128)(2,1)S(1)} %copy.232) | copy-start | bytes 786436
  327.1 35.7 %copy-start.16 = (bf16[1,4,1,2,128,128]{4,5,1,3,0,2:T(8,128)(2,1)S(1)}, bf16[1,4,1,2,128,128]{4,5,1,3,0,2:T(8,128)(2,1)}, u32[]{:S(2)}) copy-start(bf16[1,4,1,2,128,128]{4,5,1,3,0,2:T(8,128)(2,1)} %copy-done.15) | copy-start | bytes 786436
  327.1 35.7 %copy-start.18 = (bf16[1,4,1,2,128,128]{4,5,1,3,0,2:T(8,128)(2,1)S(1)}, bf16[1,4,1,2,128,128]{4,5,1,3,0,2:T(8,128)(2,1)}, u32[]{:S(2)}) copy-start(bf16[1,4,1,2,128,128]{4,5,1,3,0,2:T(8,128)(2,1)} %copy-done.17) | copy-start | bytes 786436
  341.1 24.7 %collective-permute-start.14 = (bf16[1,4,2,2,128,128]{4,5,1,3,0,2:T(8,128)(2,1)}, bf16[1,4,2,2,128,128]{4,5,1,3,0,2:T(8,128)(2,1)}, u32[]{:S(2)}, u32[]{:S(2)}) collective-permute-start(bf16[1,4,2,2,128,128]{4,5,1,3,0,2:T(8,128)(2,1)} %pad_maximum_fusion.10), channel_id=1, source_target_pairs={{0,64},{32,96},{64,0},{96,32},{1,65},{33,97},{65,1},{97,33},{2,66}... | collective-permute-start | bytes 1572872 | tf_op jit(solution)/shard_map/ppermute | solution.py:220
  343.2 70.4 %collective-permute-start = (bf16[1,4,2,2,128,128]{4,5,1,3,2,0:T(8,128)(2,1)}, bf16[1,4,2,2,128,128]{4,5,1,3,2,0:T(8,128)(2,1)S(1)}, u32[]{:S(2)}, u32[]{:S(2)}) collective-permute-start(bf16[1,4,2,2,128,128]{4,5,1,3,2,0:T(8,128)(2,1)} %pad_maximum_fusion.8), channel_id=1, source_target_pairs={{0,1},{1,2},{2,3},{3,4},{4,5},{5,6},{6,7},{7,8},{8,9},{9,10},{10,1... | collective-permute-start | bytes 1572872 | tf_op jit(solution)/shard_map/ppermute | solution.py:18
  355.5 30.6 %collective-permute-start.3 = (bf16[1,4,2,2,128,128]{4,5,1,3,2,0:T(8,128)(2,1)}, bf16[1,4,2,2,128,128]{4,5,1,3,2,0:T(8,128)(2,1)S(1)}, u32[]{:S(2)}, u32[]{:S(2)}) collective-permute-start(bf16[1,4,2,2,128,128]{4,5,1,3,2,0:T(8,128)(2,1)} %collective-permute-done.2), channel_id=1, source_target_pairs={{0,1},{1,2},{2,3},{3,4},{4,5},{5,6},{6,7},{7,8},{8,9},{9,10},{10,1... | collective-permute-start | bytes 1572872 | tf_op jit(solution)/shard_map/ppermute | solution.py:18
  357.5 59.6 %collective-permute-start.1 = (bf16[1,4,2,2,128,128]{4,5,1,3,2,0:T(8,128)(2,1)}, bf16[1,4,2,2,128,128]{4,5,1,3,2,0:T(8,128)(2,1)S(1)}, u32[]{:S(2)}, u32[]{:S(2)}) collective-permute-start(bf16[1,4,2,2,128,128]{4,5,1,3,2,0:T(8,128)(2,1)} %pad_maximum_fusion.8), channel_id=1, source_target_pairs={{1,0},{2,1},{3,2},{4,3},{5,4},{6,5},{7,6},{8,7},{9,8},{10,9},{11,1... | collective-permute-start | bytes 1572872 | tf_op jit(solution)/shard_map/ppermute | solution.py:21
  360.9 50.8 %collective-permute-start.4 = (bf16[1,4,2,2,128,128]{4,5,1,3,2,0:T(8,128)(2,1)}, bf16[1,4,2,2,128,128]{4,5,1,3,2,0:T(8,128)(2,1)S(1)}, u32[]{:S(2)}, u32[]{:S(2)}) collective-permute-start(bf16[1,4,2,2,128,128]{4,5,1,3,2,0:T(8,128)(2,1)} %collective-permute-done.2), channel_id=1, source_target_pairs={{1,0},{2,1},{3,2},{4,3},{5,4},{6,5},{7,6},{8,7},{9,8},{10,9},{11,1... | collective-permute-start | bytes 1572872 | tf_op jit(solution)/shard_map/ppermute | solution.py:21
  365.8 53.2 %copy-start.20 = (bf16[1,4,1,2,128,128]{4,5,1,3,2,0:T(8,128)(2,1)S(1)}, bf16[1,4,1,2,128,128]{4,5,1,3,2,0:T(8,128)(2,1)}, u32[]{:S(2)}) copy-start(bf16[1,4,1,2,128,128]{4,5,1,3,2,0:T(8,128)(2,1)} %copy-done.19) | copy-start | bytes 786436
  365.8 53.2 %copy-start.23 = (bf16[1,4,1,2,128,128]{4,5,1,3,2,0:T(8,128)(2,1)S(1)}, bf16[1,4,1,2,128,128]{4,5,1,3,2,0:T(8,128)(2,1)}, u32[]{:S(2)}) copy-start(bf16[1,4,1,2,128,128]{4,5,1,3,2,0:T(8,128)(2,1)} %copy-done.22) | copy-start | bytes 786436
  365.8 107.9 %collective-permute-start.11 = (bf16[2,12,2,2,128,128]{4,5,1,3,0,2:T(8,128)(2,1)}, bf16[2,12,2,2,128,128]{4,5,1,3,0,2:T(8,128)(2,1)}, u32[]{:S(2)}, u32[]{:S(2)}) collective-permute-start(bf16[2,12,2,2,128,128]{4,5,1,3,0,2:T(8,128)(2,1)} %pad_maximum_fusion.4), channel_id=1, source_target_pairs={{0,32},{32,0},{64,96},{96,64},{1,33},{33,1},{65,97},{97,65},{2,34}... | collective-permute-start | bytes 9437192 | tf_op jit(solution)/shard_map/ppermute | solution.py:224
  386.0 34.8 %collective-permute-start.15 = (bf16[1,4,2,2,128,128]{4,5,1,3,0,2:T(8,128)(2,1)}, bf16[1,4,2,2,128,128]{4,5,1,3,0,2:T(8,128)(2,1)S(1)}, u32[]{:S(2)}, u32[]{:S(2)}) collective-permute-start(bf16[1,4,2,2,128,128]{4,5,1,3,0,2:T(8,128)(2,1)} %collective-permute-done.14), channel_id=1, source_target_pairs={{0,1},{1,2},{2,3},{3,4},{4,5},{5,6},{6,7},{7,8},{8,9},{9,10},{10,1... | collective-permute-start | bytes 1572872 | tf_op jit(solution)/shard_map/ppermute | solution.py:18
  411.6 46.2 %collective-permute-start.12 = (bf16[1,4,2,2,128,128]{4,5,1,3,0,2:T(8,128)(2,1)}, bf16[1,4,2,2,128,128]{4,5,1,3,0,2:T(8,128)(2,1)}, u32[]{:S(2)}, u32[]{:S(2)}) collective-permute-start(bf16[1,4,2,2,128,128]{4,5,1,3,0,2:T(8,128)(2,1)} %pad_maximum_fusion.10), channel_id=1, source_target_pairs={{0,1},{1,2},{2,3},{3,4},{4,5},{5,6},{6,7},{7,8},{8,9},{9,10},{10,1... | collective-permute-start | bytes 1572872 | tf_op jit(solution)/shard_map/ppermute | solution.py:18
  413.7 7.2 %copy-start.38 = (bf16[1,4,2,2,128,128]{4,5,1,3,2,0:T(8,128)(2,1)}, bf16[1,4,2,2,128,128]{4,5,1,3,2,0:T(8,128)(2,1)S(1)}, u32[]{:S(2)}) copy-start(bf16[1,4,2,2,128,128]{4,5,1,3,2,0:T(8,128)(2,1)S(1)} %collective-permute-done) | copy-start | bytes 1572868
  413.7 44.2 %collective-permute-start.13 = (bf16[1,4,2,2,128,128]{4,5,1,3,0,2:T(8,128)(2,1)}, bf16[1,4,2,2,128,128]{4,5,1,3,0,2:T(8,128)(2,1)}, u32[]{:S(2)}, u32[]{:S(2)}) collective-permute-start(bf16[1,4,2,2,128,128]{4,5,1,3,0,2:T(8,128)(2,1)} %pad_maximum_fusion.10), channel_id=1, source_target_pairs={{1,0},{2,1},{3,2},{4,3},{5,4},{6,5},{7,6},{8,7},{9,8},{10,9},{11,1... | collective-permute-start | bytes 1572872 | tf_op jit(solution)/shard_map/ppermute | solution.py:21
  417.1 39.6 %collective-permute-start.16 = (bf16[1,4,2,2,128,128]{4,5,1,3,0,2:T(8,128)(2,1)}, bf16[1,4,2,2,128,128]{4,5,1,3,0,2:T(8,128)(2,1)}, u32[]{:S(2)}, u32[]{:S(2)}) collective-permute-start(bf16[1,4,2,2,128,128]{4,5,1,3,0,2:T(8,128)(2,1)} %collective-permute-done.14), channel_id=1, source_target_pairs={{1,0},{2,1},{3,2},{4,3},{5,4},{6,5},{7,6},{8,7},{9,8},{10,9},{11,1... | collective-permute-start | bytes 1572872 | tf_op jit(solution)/shard_map/ppermute | solution.py:21
  421.6 55.8 %collective-permute-start.5 = (bf16[2,12,2,2,128,128]{4,5,1,3,2,0:T(8,128)(2,1)}, bf16[2,12,2,2,128,128]{4,5,1,3,2,0:T(8,128)(2,1)}, u32[]{:S(2)}, u32[]{:S(2)}) collective-permute-start(bf16[2,12,2,2,128,128]{4,5,1,3,2,0:T(8,128)(2,1)} %pad_maximum_fusion.3), channel_id=1, source_target_pairs={{0,32},{32,0},{64,96},{96,64},{1,33},{33,1},{65,97},{97,65},{2,34}... | collective-permute-start | bytes 9437192 | tf_op jit(solution)/shard_map/ppermute | solution.py:224
  457.8 6.1 %copy-start.59 = (s32[2]{0:T(128)S(1)}, s32[2]{0:T(128)}, u32[]{:S(2)}) copy-start(s32[2]{0:T(128)} %param.23) | copy-start | bytes 28
  457.8 12.6 %copy-start.62 = (f32[2,4]{1,0:T(2,128)S(1)}, f32[2,4]{1,0:T(2,128)}, u32[]{:S(2)}) copy-start(f32[2,4]{1,0:T(2,128)} %param.20) | copy-start | bytes 100
  457.9 13.6 %copy-start.60 = (f32[2]{0:T(128)S(1)}, f32[2]{0:T(128)}, u32[]{:S(2)}) copy-start(f32[2]{0:T(128)} %param.22) | copy-start | bytes 28
  457.9 15.4 %copy-start.58 = (f32[2,128,128]{2,1,0:T(8,128)S(1)}, f32[2,128,128]{2,1,0:T(8,128)}, u32[]{:S(2)}) copy-start(f32[2,128,128]{2,1,0:T(8,128)} %param.21) | copy-start | bytes 393220
  461.5 19.6 %collective-permute-start.17 = (bf16[2,12,2,2,128,128]{4,5,1,3,0,2:T(8,128)(2,1)}, bf16[2,12,2,2,128,128]{4,5,1,3,0,2:T(8,128)(2,1)}, u32[]{:S(2)}, u32[]{:S(2)}) collective-permute-start(bf16[2,12,2,2,128,128]{4,5,1,3,0,2:T(8,128)(2,1)} %pad_maximum_fusion.5), channel_id=1, source_target_pairs={{0,32},{32,0},{64,96},{96,64},{1,33},{33,1},{65,97},{97,65},{2,34}... | collective-permute-start | bytes 9437192 | tf_op jit(solution)/shard_map/ppermute | solution.py:224
  (33 other events, 89.8 us)

commit v4 on v3

--- a/solution.py
+++ b/solution.py
@@ -118,7 +118,7 @@
     return jnp.stack([pair_value[0], pair_value[1]], axis=-3)
 
 
-def green_blocks(sigma_less, sigma_great, hamilton, slab_coupling, energies):
+def green_blocks(sigma_less, sigma_great, hamilton, slab_coupling, energies, fence=None):
     orbitals = sigma_less.shape[-1]
     slab_count = sigma_less.shape[2]
     identity = jnp.eye(orbitals, dtype=jnp.float32)
@@ -133,6 +133,8 @@
         system_re = energy_grid * identity - hamilton[:, :, slab_index] - retarded_re
         system_im = -retarded_im
         source = (lesser[:, :, 0], lesser[:, :, 1])
+        if fence is not None and slab_index == slab_count - 1:
+            fence, system_re, system_im = lax.optimization_barrier((fence, system_re, system_im))
         if slab_index > 0:
             coupling = slab_coupling[slab_index - 1]
             folded = real_right(real_left(coupling, left_ret[-1]), coupling.T)
@@ -161,10 +163,11 @@
         full_ret = add_pair(left_ret[slab_index], complex_product(bridge, left_ret[slab_index]))
         lesser_list.insert(0, full_less)
         greater_list.insert(0, greater_of(full_less, full_ret))
-    return [
+    finished = [
         jnp.stack([pack_pair(less_item), pack_pair(great_item)], axis=2).astype(jnp.bfloat16)
         for less_item, great_item in zip(lesser_list, greater_list)
     ]
+    return finished, fence
 
 
 def hamiltonian(onsite_table, cos_coupling, slab_kind, momenta_index, momenta_total):
@@ -214,7 +217,6 @@
 
 def exchange_blocks(blocks, width):
     count = lax.axis_size("kz")
-    momentum = lax.axis_index("kz")
     far_pairs = [(i, (i + 2) % count) for i in range(count)]
     near_pairs = [(i, i ^ 1) for i in range(count)]
     far = lax.ppermute(blocks, "kz", far_pairs)
@@ -223,9 +225,17 @@
     extended = jnp.concatenate([own_extended, far_extended], axis=0)
     other = lax.ppermute(extended, "kz", near_pairs)
     everyone = jnp.concatenate([extended, other], axis=0)
+    return tuple(
+        lax.slice_in_dim(everyone, index * width, (index + 1) * width, axis=1)
+        for index in range(3)
+    )
+
+
+def arrival_order():
+    count = lax.axis_size("kz")
+    momentum = lax.axis_index("kz")
     partner = momentum ^ 1
-    order = jnp.stack([momentum, (momentum + 2) % count, partner, (partner + 2) % count])
-    return everyone, order
+    return jnp.stack([momentum, (momentum + 2) % count, partner, (partner + 2) % count])
 
 
 def on_device(
@@ -250,21 +260,43 @@
     energy_index = lax.axis_index("en") * energy_local + jnp.arange(energy_local, dtype=jnp.int32)
     energies = -1.5 + 3.0 * (energy_index.astype(jnp.float32) + 0.5) / energy_total
     hamilton = hamiltonian(onsite_table, cos_coupling, slab_kind, momenta_index, momenta_total)
-    slab_blocks = green_blocks(sigma_less, sigma_great, hamilton, slab_coupling, energies)
+    chunk_count = 2 if energy_local % 2 == 0 else 1
+    chunk = energy_local // chunk_count
     table_rows = lax.dynamic_slice_in_dim(kz_table, momenta_start, momenta_local, 0)
     weights = momentum_weights(table_rows, mode_weight, momenta_total)
+    weights = jnp.take(weights, arrival_order(), axis=2)
+    pieces = []
+    previous = None
+    for chunk_index in range(chunk_count):
+        window = slice(chunk_index * chunk, (chunk_index + 1) * chunk)
+        chunk_inputs = (sigma_less[:, window], sigma_great[:, window], energies[window])
+        if previous is not None:
+            previous, chunk_inputs = lax.optimization_barrier((previous, chunk_inputs))
+        slab_blocks, fenced = green_blocks(
+            chunk_inputs[0],
+            chunk_inputs[1],
+            hamilton,
+            slab_coupling,
+            chunk_inputs[2],
+            pieces if pieces else None,
+        )
+        if fenced is not None:
+            pieces = fenced
+        previous = slab_blocks
+        pieces = pieces + [[exchange_blocks(blocks, chunk) for blocks in slab_blocks]]
     less_parts = []
     great_parts = []
-    for blocks in slab_blocks:
-        extended, order = exchange_blocks(blocks, OFFMAX)
+    for slab_index in range(len(pieces[0])):
+        extended = jnp.concatenate(
+            [
+                chunk_pieces[slab_index][side]
+                for side in range(3)
+                for chunk_pieces in pieces
+            ],
+            axis=1,
+        )
         less_part, great_part = mixed_sums(
-            extended,
-            jnp.take(weights, order, axis=2),
-            form_factor,
-            occupation,
-            energy_offset,
-            energy_local,
-            OFFMAX,
+            extended, weights, form_factor, occupation, energy_offset, energy_local, energy_local
         )
         less_parts.append(less_part.astype(jnp.bfloat16))
         great_parts.append(great_part.astype(jnp.bfloat16))

time: 515 us -> 595 us (1.16)
  starting transfers between devices: 55.6 us -> 107 us
  matrix products: 98.3 us -> 142 us
  waiting for transfers between devices: 81.7 us -> 41.8 us
  local copies, waits for them, and re-layouts: 24.9 us -> 48 us
  Pallas kernels: 191 us -> 197 us
    dot_general x116 -> x232, matrix products: 97.6 us -> 140 us  [matmul_high(): jnp.matmul(left_matrix, right_matrix, precision=lax.Precision.HIGHEST)]
    ppermute x6 -> x12, waiting for transfers between devices: 28.3 us -> 4.81 us  [padded(): lax.ppermute(lax.slice_in_dim(block, block.shape[dim] - width, None, axis...]
    ppermute x6 -> x12, starting transfers between devices: 23.2 us -> 46.4 us  [padded(): lax.ppermute(lax.slice_in_dim(block, block.shape[dim] - width, None, axis...]
    ppermute x6 -> x12, waiting for transfers between devices: 53.4 us -> 33 us  [padded(): lax.ppermute(lax.slice_in_dim(block, 0, width, axis=dim), axis, backward)]
    ppermute x6 -> x12, starting transfers between devices: 15.2 us -> 27.1 us  [padded(): lax.ppermute(lax.slice_in_dim(block, 0, width, axis=dim), axis, backward)]
    ppermute x3 -> x6, starting transfers between devices: 12.5 us -> 23.9 us  [exchange_blocks(): other = lax.ppermute(extended, 'kz', near_pairs)]
    unnamed x134 -> x193, local copies, waits for them, and re-layouts: 8.71 us -> 17.7 us
    concatenate x3 -> x6, other arithmetic: 13.6 us -> 7.16 us  [exchange_blocks(): everyone = jnp.concatenate([extended, other], axis=0)]
  transfers between devices with their start and end apart: 18 -> 36, of which waited for: 5 -> 11; matrix products, arithmetic and copies ran while one was open for 11% -> 20% of each run, Pallas kernels for 0% -> 11%
where the time goes in v4:
time: 595 us; the launch traced here: 589 us
  Pallas kernels  197 us (33%)
  matrix products  142 us (24%)
  starting transfers between devices  107 us (18%)
  local copies, waits for them, and re-layouts  48 us (8%)
  other arithmetic  43.5 us (7%)
  waiting for transfers between devices  41.8 us (7%)
  between operations  10.1 us (2%)
    pallas_call x6, Pallas kernels, hermitian_inverse(): pl.pallas_call(sweep_kernel, out_shape=(out_shape, out_shape), interpret=...  197 us
    dot_general x232, matrix products, matmul_high(): jnp.matmul(left_matrix, right_matrix, precision=lax.Precision.HIGHEST)  140 us
    ppermute x12, starting transfers between devices, padded(): lax.ppermute(lax.slice_in_dim(block, block.shape[dim] - width, None, axis...  46.4 us
    ppermute x12, waiting for transfers between devices, padded(): lax.ppermute(lax.slice_in_dim(block, 0, width, axis=dim), axis, backward)  33 us
    ppermute x12, starting transfers between devices, padded(): lax.ppermute(lax.slice_in_dim(block, 0, width, axis=dim), axis, backward)  27.1 us
    ppermute x6, starting transfers between devices, exchange_blocks(): other = lax.ppermute(extended, 'kz', near_pairs)  23.9 us
    unnamed x193, local copies, waits for them, and re-layouts  17.7 us
    reduce_sum x1, other arithmetic, mixed_sums(): jnp.sum(mode_weights * great_term[None], axis=1)  12.2 us
  transfers between devices with their start and end apart: 36, of which 11 were waited for; matrix products, arithmetic and copies ran while one was open for 20% of the time, Pallas kernels for 11%

profile of v4, /device:TPU:63, one launch (start us, length us, event | category | flops | bytes accessed | tf_op | source)
XLA Modules:
  0.0 588.8 jit_solution(13545820455352937592)
XLA Ops:
  7.5 33.0 %shard_map.122 = (f32[2,128,128]{2,1,0:T(8,128)}, f32[2,128,128]{2,1,0:T(8,128)}) custom-call(f32[2,128,128]{2,1,0:T(8,128)} %convolution_subtract_fusion.49.normal_re_ref, f32[2,128,128]{2,1,0:T(8,128)} %convolution_add_fusion.52.normal_im_ref), custom_call_target="tpu_custom_call" | custom-call | tf_op jit(solution)/shard_map/pallas_call | solution.py:98
  50.8 32.8 %shard_map.123 = (f32[2,128,128]{2,1,0:T(8,128)}, f32[2,128,128]{2,1,0:T(8,128)}) custom-call(f32[2,128,128]{2,1,0:T(8,128)} %convolution_subtract_fusion.46.normal_re_ref, f32[2,128,128]{2,1,0:T(8,128)} %convolution_add_fusion.50.normal_im_ref), custom_call_target="tpu_custom_call" | custom-call | tf_op jit(solution)/shard_map/pallas_call | solution.py:98
  95.4 32.8 %shard_map.124 = (f32[2,128,128]{2,1,0:T(8,128)}, f32[2,128,128]{2,1,0:T(8,128)}) custom-call(f32[2,128,128]{2,1,0:T(8,128)} %convolution_subtract_fusion.42.normal_re_ref, f32[2,128,128]{2,1,0:T(8,128)} %convolution_add_fusion.46.normal_im_ref), custom_call_target="tpu_custom_call" | custom-call | tf_op jit(solution)/shard_map/pallas_call | solution.py:98
  139.3 2.6 collective-permute-start.12
  141.9 2.7 collective-permute-start.13
  156.4 2.9 collective-permute-start.8
  179.6 32.8 %shard_map.125 = (f32[2,128,128]{2,1,0:T(8,128)}, f32[2,128,128]{2,1,0:T(8,128)}) custom-call(f32[2,128,128]{2,1,0:T(8,128)} %convolution_subtract_fusion.28.normal_re_ref, f32[2,128,128]{2,1,0:T(8,128)} %convolution_add_fusion.31.normal_im_ref), custom_call_target="tpu_custom_call" | custom-call | tf_op jit(solution)/shard_map/pallas_call | solution.py:98
  221.9 32.8 %shard_map.126 = (f32[2,128,128]{2,1,0:T(8,128)}, f32[2,128,128]{2,1,0:T(8,128)}) custom-call(f32[2,128,128]{2,1,0:T(8,128)} %convolution_subtract_fusion.25.normal_re_ref, f32[2,128,128]{2,1,0:T(8,128)} %convolution_add_fusion.29.normal_im_ref), custom_call_target="tpu_custom_call" | custom-call | tf_op jit(solution)/shard_map/pallas_call | solution.py:98
  275.4 5.8 collective-permute-start.15
  281.3 1.9 collective-permute-start.16
  285.3 7.0 %collective-permute-start.6 = (bf16[1,2,2,2,128,128]{4,5,1,3,0,2:T(8,128)(2,1)}, bf16[1,2,2,2,128,128]{4,5,1,3,0,2:T(8,128)(2,1)S(1)}, u32[]{:S(2)}, u32[]{:S(2)}) collective-permute-start(bf16[1,2,2,2,128,128]{4,5,1,3,0,2:T(8,128)(2,1)} %pad_maximum_fusion.15), channel_id=1, source_target_pairs={{0,1},{1,2},{2,3},{3,4},{4,5},{5,6},{6,7},{7,8},{8,9},{9,10},{10,1... | collective-permute-start | bytes 786440 | tf_op jit(solution)/shard_map/ppermute | solution.py:18
  296.2 3.4 collective-permute-start.10
  299.6 2.3 pad_maximum_fusion.8
  302.0 6.2 %collective-permute-start.17 = (bf16[2,6,2,2,128,128]{4,5,1,3,0,2:T(8,128)(2,1)}, bf16[2,6,2,2,128,128]{4,5,1,3,0,2:T(8,128)(2,1)}, u32[]{:S(2)}, u32[]{:S(2)}) collective-permute-start(bf16[2,6,2,2,128,128]{4,5,1,3,0,2:T(8,128)(2,1)} %pad_maximum_fusion.8), channel_id=1, source_target_pairs={{0,32},{32,0},{64,96},{96,64},{1,33},{33,1},{65,97},{97,65},{2,34}... | collective-permute-start | bytes 4718600 | tf_op jit(solution)/shard_map/ppermute | solution.py:226
  311.1 6.4 %collective-permute-start = (bf16[1,2,2,2,128,128]{4,5,1,3,2,0:T(8,128)(2,1)}, bf16[1,2,2,2,128,128]{4,5,1,3,2,0:T(8,128)(2,1)S(1)}, u32[]{:S(2)}, u32[]{:S(2)}) collective-permute-start(bf16[1,2,2,2,128,128]{4,5,1,3,2,0:T(8,128)(2,1)} %pad_maximum_fusion.14), channel_id=1, source_target_pairs={{0,1},{1,2},{2,3},{3,4},{4,5},{5,6},{6,7},{7,8},{8,9},{9,10},{10,1... | collective-permute-start | bytes 786440 | tf_op jit(solution)/shard_map/ppermute | solution.py:18
  317.5 1.9 collective-permute-start.3
  321.1 9.9 %collective-permute-start.11 = (bf16[2,6,2,2,128,128]{4,5,1,3,0,2:T(8,128)(2,1)}, bf16[2,6,2,2,128,128]{4,5,1,3,0,2:T(8,128)(2,1)}, u32[]{:S(2)}, u32[]{:S(2)}) collective-permute-start(bf16[2,6,2,2,128,128]{4,5,1,3,0,2:T(8,128)(2,1)} %pad_maximum_fusion.7), channel_id=1, source_target_pairs={{0,32},{32,0},{64,96},{96,64},{1,33},{33,1},{65,97},{97,65},{2,34}... | collective-permute-start | bytes 4718600 | tf_op jit(solution)/shard_map/ppermute | solution.py:226
  333.6 1.9 collective-permute-start.1
  335.6 8.3 %collective-permute-done.4 = bf16[1,2,2,2,128,128]{4,5,1,3,2,0:T(8,128)(2,1)S(1)} collective-permute-done((bf16[1,2,2,2,128,128]{4,5,1,3,2,0:T(8,128)(2,1)S(1)}, bf16[1,2,2,2,128,128]{4,5,1,3,2,0:T(8,128)(2,1)S(1)}, u32[]{:S(2)}, u32[]{:S(2)}) %collective-permute-start.4) | collective-permute-done | bytes 262176 | tf_op jit(solution)/shard_map/ppermute | solution.py:21
  343.9 5.6 collective-permute-done.1
  359.3 1.9 pad_maximum_fusion.2
  373.5 32.8 %shard_map.127 = (f32[2,128,128]{2,1,0:T(8,128)}, f32[2,128,128]{2,1,0:T(8,128)}) custom-call(f32[2,128,128]{2,1,0:T(8,128)} %convolution_subtract_fusion.21.normal_re_ref, f32[2,128,128]{2,1,0:T(8,128)} %convolution_add_fusion.25.normal_im_ref), custom_call_target="tpu_custom_call" | custom-call | tf_op jit(solution)/shard_map/pallas_call | solution.py:98
  431.0 2.0 fusion.20
  434.7 2.0 fusion.23
  453.7 1.9 collective-permute-start.24
  455.7 3.8 collective-permute-start.25
  480.4 2.1 convert_bitcast_fusion.5
  485.9 2.4 collective-permute-start.20
  489.3 4.3 collective-permute-start.27
  494.6 1.9 collective-permute-start.28
  497.5 6.4 %collective-permute-start.18 = (bf16[1,2,2,2,128,128]{4,5,1,3,2,0:T(8,128)(2,1)}, bf16[1,2,2,2,128,128]{4,5,1,3,2,0:T(8,128)(2,1)S(1)}, u32[]{:S(2)}, u32[]{:S(2)}) collective-permute-start(bf16[1,2,2,2,128,128]{4,5,1,3,2,0:T(8,128)(2,1)} %pad_maximum_fusion.17), channel_id=1, source_target_pairs={{0,1},{1,2},{2,3},{3,4},{4,5},{5,6},{6,7},{7,8},{8,9},{9,10},{10,1... | collective-permute-start | bytes 786440 | tf_op jit(solution)/shard_map/ppermute | solution.py:18
  503.9 2.3 collective-permute-start.21
  510.5 2.5 collective-permute-start.29
  516.8 1.9 collective-permute-start.19
  519.9 4.0 collective-permute-done.32
  523.8 4.1 collective-permute-start.30
  528.0 2.6 collective-permute-done.22
  532.6 3.6 collective-permute-done.19
  536.4 2.4 collective-permute-start.23
  538.9 1.9 collective-permute-start.34
  540.9 3.5 collective-permute-done.33
  544.5 1.9 collective-permute-start.31
  546.5 6.6 %collective-permute-done.34 = bf16[1,2,2,2,128,128]{4,5,1,3,0,2:T(8,128)(2,1)S(1)} collective-permute-done((bf16[1,2,2,2,128,128]{4,5,1,3,0,2:T(8,128)(2,1)S(1)}, bf16[1,2,2,2,128,128]{4,5,1,3,0,2:T(8,128)(2,1)S(1)}, u32[]{:S(2)}, u32[]{:S(2)}) %collective-permute-start.34) | collective-permute-done | bytes 262176 | tf_op jit(solution)/shard_map/ppermute | solution.py:21
  553.1 5.1 collective-permute-done.31
  558.4 2.1 collective-permute-start.35
  566.1 2.2 copy-done.3
  571.0 12.2 %fusion.1 = (f32[4,2,128,128]{2,3,0,1:T(8,128)S(1)}, f32[4,2,128,128]{2,3,0,1:T(8,128)S(1)}, f32[4,2,128,128]{2,3,0,1:T(8,128)S(1)}, f32[4,2,128,128]{2,3,0,1:T(...) fusion(bf16[4,12,2,2,128,128]{4,5,1,3,0,2:T(8,128)(2,1)S(1)} %s, ...), kind=kLoop, calls=%fused_computation.10 | loop fusion | flops 42467328 | bytes 31457348 | tf_op jit(solution)/shard_map/reduce_sum | solution.py:212
  583.2 2.9 fusion.57
  (584 shorter events, 222.5 us)
Async XLA Ops:
  7.5 38.7 %copy-start.2 = (f32[2,128,128]{2,1,0:T(8,128)S(1)}, f32[2,128,128]{2,1,0:T(8,128)}, u32[]{:S(2)}) copy-start(f32[2,128,128]{2,1,0:T(8,128)} %param.15) | copy-start | bytes 393220
  137.4 162.1 %copy-start.32 = (bf16[1,2,1,2,128,128]{4,5,1,3,0,2:T(8,128)(2,1)}, bf16[1,2,1,2,128,128]{4,5,1,3,0,2:T(8,128)(2,1)S(1)}, u32[]{:S(2)}) copy-start(bf16[1,2,1,2,128,128]{4,5,1,3,0,2:T(8,128)(2,1)S(1)} %maximum_bitcast_fusion.5) | copy-start | bytes 393220
  138.2 137.2 %collective-permute-start.14 = (bf16[1,2,2,2,128,128]{4,5,1,3,0,2:T(8,128)(2,1)}, bf16[1,2,2,2,128,128]{4,5,1,3,0,2:T(8,128)(2,1)}, u32[]{:S(2)}, u32[]{:S(2)}) collective-permute-start(bf16[1,2,2,2,128,128]{4,5,1,3,0,2:T(8,128)(2,1)} %pad_maximum_fusion.16), channel_id=1, source_target_pairs={{0,64},{32,96},{64,0},{96,32},{1,65},{33,97},{65,1},{97,33},{2,66}... | collective-permute-start | bytes 786440 | tf_op jit(solution)/shard_map/ppermute | solution.py:222
  139.3 156.9 %collective-permute-start.12 = (bf16[1,2,2,2,128,128]{4,5,1,3,0,2:T(8,128)(2,1)}, bf16[1,2,2,2,128,128]{4,5,1,3,0,2:T(8,128)(2,1)}, u32[]{:S(2)}, u32[]{:S(2)}) collective-permute-start(bf16[1,2,2,2,128,128]{4,5,1,3,0,2:T(8,128)(2,1)} %pad_maximum_fusion.16), channel_id=1, source_target_pairs={{0,1},{1,2},{2,3},{3,4},{4,5},{5,6},{6,7},{7,8},{8,9},{9,10},{10,1... | collective-permute-start | bytes 786440 | tf_op jit(solution)/shard_map/ppermute | solution.py:18
  141.9 157.7 %collective-permute-start.13 = (bf16[1,2,2,2,128,128]{4,5,1,3,0,2:T(8,128)(2,1)}, bf16[1,2,2,2,128,128]{4,5,1,3,0,2:T(8,128)(2,1)}, u32[]{:S(2)}, u32[]{:S(2)}) collective-permute-start(bf16[1,2,2,2,128,128]{4,5,1,3,0,2:T(8,128)(2,1)} %pad_maximum_fusion.16), channel_id=1, source_target_pairs={{1,0},{2,1},{3,2},{4,3},{5,4},{6,5},{7,6},{8,7},{9,8},{10,9},{11,1... | collective-permute-start | bytes 786440 | tf_op jit(solution)/shard_map/ppermute | solution.py:21
  155.3 164.4 %copy-start.33 = (bf16[1,2,1,2,128,128]{4,5,1,3,0,2:T(8,128)(2,1)}, bf16[1,2,1,2,128,128]{4,5,1,3,0,2:T(8,128)(2,1)S(1)}, u32[]{:S(2)}) copy-start(bf16[1,2,1,2,128,128]{4,5,1,3,0,2:T(8,128)(2,1)S(1)} %copy.319) | copy-start | bytes 393220
  155.6 164.1 %copy-start.35 = (bf16[1,2,1,2,128,128]{4,5,1,3,0,2:T(8,128)(2,1)}, bf16[1,2,1,2,128,128]{4,5,1,3,0,2:T(8,128)(2,1)S(1)}, u32[]{:S(2)}) copy-start(bf16[1,2,1,2,128,128]{4,5,1,3,0,2:T(8,128)(2,1)S(1)} %maximum_bitcast_fusion.3) | copy-start | bytes 393220
  156.4 136.9 %collective-permute-start.8 = (bf16[1,2,2,2,128,128]{4,5,1,3,0,2:T(8,128)(2,1)}, bf16[1,2,2,2,128,128]{4,5,1,3,0,2:T(8,128)(2,1)}, u32[]{:S(2)}, u32[]{:S(2)}) collective-permute-start(bf16[1,2,2,2,128,128]{4,5,1,3,0,2:T(8,128)(2,1)} %pad_maximum_fusion.15), channel_id=1, source_target_pairs={{0,64},{32,96},{64,0},{96,32},{1,65},{33,97},{65,1},{97,33},{2,66}... | collective-permute-start | bytes 786440 | tf_op jit(solution)/shard_map/ppermute | solution.py:222
  275.4 9.9 %collective-permute-start.15 = (bf16[1,2,2,2,128,128]{4,5,1,3,0,2:T(8,128)(2,1)}, bf16[1,2,2,2,128,128]{4,5,1,3,0,2:T(8,128)(2,1)S(1)}, u32[]{:S(2)}, u32[]{:S(2)}) collective-permute-start(bf16[1,2,2,2,128,128]{4,5,1,3,0,2:T(8,128)(2,1)} %collective-permute-done.14), channel_id=1, source_target_pairs={{0,1},{1,2},{2,3},{3,4},{4,5},{5,6},{6,7},{7,8},{8,9},{9,10},{10,1... | collective-permute-start | bytes 786440 | tf_op jit(solution)/shard_map/ppermute | solution.py:18
  281.3 13.0 %collective-permute-start.16 = (bf16[1,2,2,2,128,128]{4,5,1,3,0,2:T(8,128)(2,1)}, bf16[1,2,2,2,128,128]{4,5,1,3,0,2:T(8,128)(2,1)S(1)}, u32[]{:S(2)}, u32[]{:S(2)}) collective-permute-start(bf16[1,2,2,2,128,128]{4,5,1,3,0,2:T(8,128)(2,1)} %collective-permute-done.14), channel_id=1, source_target_pairs={{1,0},{2,1},{3,2},{4,3},{5,4},{6,5},{7,6},{8,7},{9,8},{10,9},{11,1... | collective-permute-start | bytes 786440 | tf_op jit(solution)/shard_map/ppermute | solution.py:21
  285.3 34.2 %collective-permute-start.6 = (bf16[1,2,2,2,128,128]{4,5,1,3,0,2:T(8,128)(2,1)}, bf16[1,2,2,2,128,128]{4,5,1,3,0,2:T(8,128)(2,1)S(1)}, u32[]{:S(2)}, u32[]{:S(2)}) collective-permute-start(bf16[1,2,2,2,128,128]{4,5,1,3,0,2:T(8,128)(2,1)} %pad_maximum_fusion.15), channel_id=1, source_target_pairs={{0,1},{1,2},{2,3},{3,4},{4,5},{5,6},{6,7},{7,8},{8,9},{9,10},{10,1... | collective-permute-start | bytes 786440 | tf_op jit(solution)/shard_map/ppermute | solution.py:18
  293.3 17.7 %collective-permute-start.2 = (bf16[1,2,2,2,128,128]{4,5,1,3,2,0:T(8,128)(2,1)}, bf16[1,2,2,2,128,128]{4,5,1,3,2,0:T(8,128)(2,1)S(1)}, u32[]{:S(2)}, u32[]{:S(2)}) collective-permute-start(bf16[1,2,2,2,128,128]{4,5,1,3,2,0:T(8,128)(2,1)} %pad_maximum_fusion.14), channel_id=1, source_target_pairs={{0,64},{32,96},{64,0},{96,32},{1,65},{33,97},{65,1},{97,33},{2,66}... | collective-permute-start | bytes 786440 | tf_op jit(solution)/shard_map/ppermute | solution.py:222
  294.2 13.9 %collective-permute-start.9 = (bf16[1,2,2,2,128,128]{4,5,1,3,0,2:T(8,128)(2,1)}, bf16[1,2,2,2,128,128]{4,5,1,3,0,2:T(8,128)(2,1)S(1)}, u32[]{:S(2)}, u32[]{:S(2)}) collective-permute-start(bf16[1,2,2,2,128,128]{4,5,1,3,0,2:T(8,128)(2,1)} %collective-permute-done.8), channel_id=1, source_target_pairs={{0,1},{1,2},{2,3},{3,4},{4,5},{5,6},{6,7},{7,8},{8,9},{9,10},{10,1... | collective-permute-start | bytes 786440 | tf_op jit(solution)/shard_map/ppermute | solution.py:18
  296.2 21.2 %collective-permute-start.10 = (bf16[1,2,2,2,128,128]{4,5,1,3,0,2:T(8,128)(2,1)}, bf16[1,2,2,2,128,128]{4,5,1,3,0,2:T(8,128)(2,1)S(1)}, u32[]{:S(2)}, u32[]{:S(2)}) collective-permute-start(bf16[1,2,2,2,128,128]{4,5,1,3,0,2:T(8,128)(2,1)} %collective-permute-done.8), channel_id=1, source_target_pairs={{1,0},{2,1},{3,2},{4,3},{5,4},{6,5},{7,6},{8,7},{9,8},{10,9},{11,1... | collective-permute-start | bytes 786440 | tf_op jit(solution)/shard_map/ppermute | solution.py:21
  302.0 57.3 %collective-permute-start.17 = (bf16[2,6,2,2,128,128]{4,5,1,3,0,2:T(8,128)(2,1)}, bf16[2,6,2,2,128,128]{4,5,1,3,0,2:T(8,128)(2,1)}, u32[]{:S(2)}, u32[]{:S(2)}) collective-permute-start(bf16[2,6,2,2,128,128]{4,5,1,3,0,2:T(8,128)(2,1)} %pad_maximum_fusion.8), channel_id=1, source_target_pairs={{0,32},{32,0},{64,96},{96,64},{1,33},{33,1},{65,97},{97,65},{2,34}... | collective-permute-start | bytes 4718600 | tf_op jit(solution)/shard_map/ppermute | solution.py:226
  308.1 11.6 %collective-permute-start.7 = (bf16[1,2,2,2,128,128]{4,5,1,3,0,2:T(8,128)(2,1)}, bf16[1,2,2,2,128,128]{4,5,1,3,0,2:T(8,128)(2,1)S(1)}, u32[]{:S(2)}, u32[]{:S(2)}) collective-permute-start(bf16[1,2,2,2,128,128]{4,5,1,3,0,2:T(8,128)(2,1)} %pad_maximum_fusion.15), channel_id=1, source_target_pairs={{1,0},{2,1},{3,2},{4,3},{5,4},{6,5},{7,6},{8,7},{9,8},{10,9},{11,1... | collective-permute-start | bytes 786440 | tf_op jit(solution)/shard_map/ppermute | solution.py:21
  310.1 22.9 %copy-start.79 = (s32[2]{0:T(128)S(1)}, s32[2]{0:T(128)}, u32[]{:S(2)}) copy-start(s32[2]{0:T(128)} %param.21) | copy-start | bytes 28
  311.1 32.8 %collective-permute-start = (bf16[1,2,2,2,128,128]{4,5,1,3,2,0:T(8,128)(2,1)}, bf16[1,2,2,2,128,128]{4,5,1,3,2,0:T(8,128)(2,1)S(1)}, u32[]{:S(2)}, u32[]{:S(2)}) collective-permute-start(bf16[1,2,2,2,128,128]{4,5,1,3,2,0:T(8,128)(2,1)} %pad_maximum_fusion.14), channel_id=1, source_target_pairs={{0,1},{1,2},{2,3},{3,4},{4,5},{5,6},{6,7},{7,8},{8,9},{9,10},{10,1... | collective-permute-start | bytes 786440 | tf_op jit(solution)/shard_map/ppermute | solution.py:18
  317.5 16.1 %collective-permute-start.3 = (bf16[1,2,2,2,128,128]{4,5,1,3,2,0:T(8,128)(2,1)S(1)}, bf16[1,2,2,2,128,128]{4,5,1,3,2,0:T(8,128)(2,1)S(1)}, u32[]{:S(2)}, u32[]{:S(2)}) collective-permute-start(bf16[1,2,2,2,128,128]{4,5,1,3,2,0:T(8,128)(2,1)S(1)} %collective-permute-done.2), channel_id=1, source_target_pairs={{0,1},{1,2},{2,3},{3,4},{4,5},{5,6},{6,7},{7,8},{8,9},{9,10},{10,1... | collective-permute-start | bytes 786440 | tf_op jit(solution)/shard_map/ppermute | solution.py:18
  319.4 30.1 %copy-start.38 = (bf16[1,2,1,2,128,128]{4,5,1,3,2,0:T(8,128)(2,1)S(1)}, bf16[1,2,1,2,128,128]{4,5,1,3,2,0:T(8,128)(2,1)}, u32[]{:S(2)}) copy-start(bf16[1,2,1,2,128,128]{4,5,1,3,2,0:T(8,128)(2,1)} %copy-done.37) | copy-start | bytes 393220
  319.4 30.1 %copy-start.41 = (bf16[1,2,1,2,128,128]{4,5,1,3,2,0:T(8,128)(2,1)S(1)}, bf16[1,2,1,2,128,128]{4,5,1,3,2,0:T(8,128)(2,1)}, u32[]{:S(2)}) copy-start(bf16[1,2,1,2,128,128]{4,5,1,3,2,0:T(8,128)(2,1)} %copy-done.40) | copy-start | bytes 393220
  321.1 42.0 %collective-permute-start.11 = (bf16[2,6,2,2,128,128]{4,5,1,3,0,2:T(8,128)(2,1)}, bf16[2,6,2,2,128,128]{4,5,1,3,0,2:T(8,128)(2,1)}, u32[]{:S(2)}, u32[]{:S(2)}) collective-permute-start(bf16[2,6,2,2,128,128]{4,5,1,3,0,2:T(8,128)(2,1)} %pad_maximum_fusion.7), channel_id=1, source_target_pairs={{0,32},{32,0},{64,96},{96,64},{1,33},{33,1},{65,97},{97,65},{2,34}... | collective-permute-start | bytes 4718600 | tf_op jit(solution)/shard_map/ppermute | solution.py:226
  331.0 12.8 %collective-permute-start.4 = (bf16[1,2,2,2,128,128]{4,5,1,3,2,0:T(8,128)(2,1)S(1)}, bf16[1,2,2,2,128,128]{4,5,1,3,2,0:T(8,128)(2,1)S(1)}, u32[]{:S(2)}, u32[]{:S(2)}) collective-permute-start(bf16[1,2,2,2,128,128]{4,5,1,3,2,0:T(8,128)(2,1)S(1)} %collective-permute-done.2), channel_id=1, source_target_pairs={{1,0},{2,1},{3,2},{4,3},{5,4},{6,5},{7,6},{8,7},{9,8},{10,9},{11,1... | collective-permute-start | bytes 786440 | tf_op jit(solution)/shard_map/ppermute | solution.py:21
  333.6 15.9 %collective-permute-start.1 = (bf16[1,2,2,2,128,128]{4,5,1,3,2,0:T(8,128)(2,1)}, bf16[1,2,2,2,128,128]{4,5,1,3,2,0:T(8,128)(2,1)S(1)}, u32[]{:S(2)}, u32[]{:S(2)}) collective-permute-start(bf16[1,2,2,2,128,128]{4,5,1,3,2,0:T(8,128)(2,1)} %pad_maximum_fusion.14), channel_id=1, source_target_pairs={{1,0},{2,1},{3,2},{4,3},{5,4},{6,5},{7,6},{8,7},{9,8},{10,9},{11,1... | collective-permute-start | bytes 786440 | tf_op jit(solution)/shard_map/ppermute | solution.py:21
  350.9 15.6 %collective-permute-start.5 = (bf16[2,6,2,2,128,128]{4,5,1,3,2,0:T(8,128)(2,1)}, bf16[2,6,2,2,128,128]{4,5,1,3,2,0:T(8,128)(2,1)}, u32[]{:S(2)}, u32[]{:S(2)}) collective-permute-start(bf16[2,6,2,2,128,128]{4,5,1,3,2,0:T(8,128)(2,1)} %pad_maximum_fusion.6), channel_id=1, source_target_pairs={{0,32},{32,0},{64,96},{96,64},{1,33},{33,1},{65,97},{97,65},{2,34}... | collective-permute-start | bytes 4718600 | tf_op jit(solution)/shard_map/ppermute | solution.py:226
  441.4 19.3 %copy-start.23 = (f32[2,128,128]{1,2,0:T(8,128)S(1)}, f32[2,128,128]{1,2,0:T(8,128)}, u32[]{:S(2)}) copy-start(f32[2,128,128]{1,2,0:T(8,128)} %fusion.20) | copy-start | bytes 393220
  445.6 17.2 %copy-start.14 = (f32[2,128,128]{2,1,0:T(8,128)S(1)}, f32[2,128,128]{2,1,0:T(8,128)}, u32[]{:S(2)}) copy-start(f32[2,128,128]{2,1,0:T(8,128)} %copy-done.13) | copy-start | bytes 393220
  453.2 36.1 %collective-permute-start.26 = (bf16[1,2,2,2,128,128]{4,5,1,3,0,2:T(8,128)(2,1)}, bf16[1,2,2,2,128,128]{4,5,1,3,0,2:T(8,128)(2,1)}, u32[]{:S(2)}, u32[]{:S(2)}) collective-permute-start(bf16[1,2,2,2,128,128]{4,5,1,3,0,2:T(8,128)(2,1)} %pad_maximum_fusion.18), channel_id=1, source_target_pairs={{0,64},{32,96},{64,0},{96,32},{1,65},{33,97},{65,1},{97,33},{2,66}... | collective-permute-start | bytes 786440 | tf_op jit(solution)/shard_map/ppermute | solution.py:222
  453.7 55.5 %collective-permute-start.24 = (bf16[1,2,2,2,128,128]{4,5,1,3,0,2:T(8,128)(2,1)}, bf16[1,2,2,2,128,128]{4,5,1,3,0,2:T(8,128)(2,1)}, u32[]{:S(2)}, u32[]{:S(2)}) collective-permute-start(bf16[1,2,2,2,128,128]{4,5,1,3,0,2:T(8,128)(2,1)} %pad_maximum_fusion.18), channel_id=1, source_target_pairs={{0,1},{1,2},{2,3},{3,4},{4,5},{5,6},{6,7},{7,8},{8,9},{9,10},{10,1... | collective-permute-start | bytes 786440 | tf_op jit(solution)/shard_map/ppermute | solution.py:18
  455.7 53.5 %collective-permute-start.25 = (bf16[1,2,2,2,128,128]{4,5,1,3,0,2:T(8,128)(2,1)}, bf16[1,2,2,2,128,128]{4,5,1,3,0,2:T(8,128)(2,1)}, u32[]{:S(2)}, u32[]{:S(2)}) collective-permute-start(bf16[1,2,2,2,128,128]{4,5,1,3,0,2:T(8,128)(2,1)} %pad_maximum_fusion.18), channel_id=1, source_target_pairs={{1,0},{2,1},{3,2},{4,3},{5,4},{6,5},{7,6},{8,7},{9,8},{10,9},{11,1... | collective-permute-start | bytes 786440 | tf_op jit(solution)/shard_map/ppermute | solution.py:21
  485.9 23.3 %copy-start.44 = (bf16[1,2,1,2,128,128]{4,5,1,3,0,2:T(8,128)(2,1)S(1)}, bf16[1,2,1,2,128,128]{4,5,1,3,0,2:T(8,128)(2,1)}, u32[]{:S(2)}) copy-start(bf16[1,2,1,2,128,128]{4,5,1,3,0,2:T(8,128)(2,1)} %copy-done.43) | copy-start | bytes 393220
  485.9 23.3 %copy-start.46 = (bf16[1,2,1,2,128,128]{4,5,1,3,0,2:T(8,128)(2,1)S(1)}, bf16[1,2,1,2,128,128]{4,5,1,3,0,2:T(8,128)(2,1)}, u32[]{:S(2)}) copy-start(bf16[1,2,1,2,128,128]{4,5,1,3,0,2:T(8,128)(2,1)} %copy-done.45) | copy-start | bytes 393220
  485.9 11.6 %collective-permute-start.20 = (bf16[1,2,2,2,128,128]{4,5,1,3,2,0:T(8,128)(2,1)}, bf16[1,2,2,2,128,128]{4,5,1,3,2,0:T(8,128)(2,1)}, u32[]{:S(2)}, u32[]{:S(2)}) collective-permute-start(bf16[1,2,2,2,128,128]{4,5,1,3,2,0:T(8,128)(2,1)} %pad_maximum_fusion.17), channel_id=1, source_target_pairs={{0,64},{32,96},{64,0},{96,32},{1,65},{33,97},{65,1},{97,33},{2,66}... | collective-permute-start | bytes 786440 | tf_op jit(solution)/shard_map/ppermute | solution.py:222
  489.3 14.7 %collective-permute-start.27 = (bf16[1,2,2,2,128,128]{4,5,1,3,0,2:T(8,128)(2,1)}, bf16[1,2,2,2,128,128]{4,5,1,3,0,2:T(8,128)(2,1)S(1)}, u32[]{:S(2)}, u32[]{:S(2)}) collective-permute-start(bf16[1,2,2,2,128,128]{4,5,1,3,0,2:T(8,128)(2,1)} %collective-permute-done.26), channel_id=1, source_target_pairs={{0,1},{1,2},{2,3},{3,4},{4,5},{5,6},{6,7},{7,8},{8,9},{9,10},{10,1... | collective-permute-start | bytes 786440 | tf_op jit(solution)/shard_map/ppermute | solution.py:18
  494.6 13.6 %collective-permute-start.28 = (bf16[1,2,2,2,128,128]{4,5,1,3,0,2:T(8,128)(2,1)}, bf16[1,2,2,2,128,128]{4,5,1,3,0,2:T(8,128)(2,1)}, u32[]{:S(2)}, u32[]{:S(2)}) collective-permute-start(bf16[1,2,2,2,128,128]{4,5,1,3,0,2:T(8,128)(2,1)} %collective-permute-done.26), channel_id=1, source_target_pairs={{1,0},{2,1},{3,2},{4,3},{5,4},{6,5},{7,6},{8,7},{9,8},{10,9},{11,1... | collective-permute-start | bytes 786440 | tf_op jit(solution)/shard_map/ppermute | solution.py:21
  497.5 35.0 %collective-permute-start.18 = (bf16[1,2,2,2,128,128]{4,5,1,3,2,0:T(8,128)(2,1)}, bf16[1,2,2,2,128,128]{4,5,1,3,2,0:T(8,128)(2,1)S(1)}, u32[]{:S(2)}, u32[]{:S(2)}) collective-permute-start(bf16[1,2,2,2,128,128]{4,5,1,3,2,0:T(8,128)(2,1)} %pad_maximum_fusion.17), channel_id=1, source_target_pairs={{0,1},{1,2},{2,3},{3,4},{4,5},{5,6},{6,7},{7,8},{8,9},{9,10},{10,1... | collective-permute-start | bytes 786440 | tf_op jit(solution)/shard_map/ppermute | solution.py:18
  503.9 12.9 %collective-permute-start.21 = (bf16[1,2,2,2,128,128]{4,5,1,3,2,0:T(8,128)(2,1)}, bf16[1,2,2,2,128,128]{4,5,1,3,2,0:T(8,128)(2,1)S(1)}, u32[]{:S(2)}, u32[]{:S(2)}) collective-permute-start(bf16[1,2,2,2,128,128]{4,5,1,3,2,0:T(8,128)(2,1)} %collective-permute-done.20), channel_id=1, source_target_pairs={{0,1},{1,2},{2,3},{3,4},{4,5},{5,6},{6,7},{7,8},{8,9},{9,10},{10,1... | collective-permute-start | bytes 786440 | tf_op jit(solution)/shard_map/ppermute | solution.py:18
  510.5 50.0 %collective-permute-start.29 = (bf16[2,6,2,2,128,128]{4,5,1,3,0,2:T(8,128)(2,1)S(1)}, bf16[2,6,2,2,128,128]{4,5,1,3,0,2:T(8,128)(2,1)S(1)}, u32[]{:S(2)}, u32[]{:S(2)}) collective-permute-start(bf16[2,6,2,2,128,128]{4,5,1,3,0,2:T(8,128)(2,1)S(1)} %pad_maximum_fusion.10), channel_id=1, source_target_pairs={{0,32},{32,0},{64,96},{96,64},{1,33},{33,1},{65,97},{97,65},{2,34}... | collective-permute-start | bytes 4718600 | tf_op jit(solution)/shard_map/ppermute | solution.py:226
  513.0 10.9 %collective-permute-start.32 = (bf16[1,2,2,2,128,128]{4,5,1,3,0,2:T(8,128)(2,1)S(1)}, bf16[1,2,2,2,128,128]{4,5,1,3,0,2:T(8,128)(2,1)S(1)}, u32[]{:S(2)}, u32[]{:S(2)}) collective-permute-start(bf16[1,2,2,2,128,128]{4,5,1,3,0,2:T(8,128)(2,1)S(1)} %pad_maximum_fusion.19), channel_id=1, source_target_pairs={{0,64},{32,96},{64,0},{96,32},{1,65},{33,97},{65,1},{97,33},{2,66}... | collective-permute-start | bytes 786440 | tf_op jit(solution)/shard_map/ppermute | solution.py:222
  514.8 15.8 %collective-permute-start.22 = (bf16[1,2,2,2,128,128]{4,5,1,3,2,0:T(8,128)(2,1)}, bf16[1,2,2,2,128,128]{4,5,1,3,2,0:T(8,128)(2,1)S(1)}, u32[]{:S(2)}, u32[]{:S(2)}) collective-permute-start(bf16[1,2,2,2,128,128]{4,5,1,3,2,0:T(8,128)(2,1)} %collective-permute-done.20), channel_id=1, source_target_pairs={{1,0},{2,1},{3,2},{4,3},{5,4},{6,5},{7,6},{8,7},{9,8},{10,9},{11,1... | collective-permute-start | bytes 786440 | tf_op jit(solution)/shard_map/ppermute | solution.py:21
  516.8 19.3 %collective-permute-start.19 = (bf16[1,2,2,2,128,128]{4,5,1,3,2,0:T(8,128)(2,1)}, bf16[1,2,2,2,128,128]{4,5,1,3,2,0:T(8,128)(2,1)S(1)}, u32[]{:S(2)}, u32[]{:S(2)}) collective-permute-start(bf16[1,2,2,2,128,128]{4,5,1,3,2,0:T(8,128)(2,1)} %pad_maximum_fusion.17), channel_id=1, source_target_pairs={{1,0},{2,1},{3,2},{4,3},{5,4},{6,5},{7,6},{8,7},{9,8},{10,9},{11,1... | collective-permute-start | bytes 786440 | tf_op jit(solution)/shard_map/ppermute | solution.py:21
  518.8 20.0 %copy-start.9 = (bf16[4,2,2,2,128,128]{4,5,1,3,2,0:T(8,128)(2,1)S(1)}, bf16[4,2,2,2,128,128]{4,5,1,3,2,0:T(8,128)(2,1)}, u32[]{:S(2)}) copy-start(bf16[4,2,2,2,128,128]{4,5,1,3,2,0:T(8,128)(2,1)} %get-tuple-element.37) | copy-start | bytes 3145732
  523.8 29.2 %collective-permute-start.30 = (bf16[1,2,2,2,128,128]{4,5,1,3,0,2:T(8,128)(2,1)S(1)}, bf16[1,2,2,2,128,128]{4,5,1,3,0,2:T(8,128)(2,1)S(1)}, u32[]{:S(2)}, u32[]{:S(2)}) collective-permute-start(bf16[1,2,2,2,128,128]{4,5,1,3,0,2:T(8,128)(2,1)S(1)} %pad_maximum_fusion.19), channel_id=1, source_target_pairs={{0,1},{1,2},{2,3},{3,4},{4,5},{5,6},{6,7},{7,8},{8,9},{9,10},{10,1... | collective-permute-start | bytes 786440 | tf_op jit(solution)/shard_map/ppermute | solution.py:18
  530.6 13.9 %collective-permute-start.33 = (bf16[1,2,2,2,128,128]{4,5,1,3,0,2:T(8,128)(2,1)S(1)}, bf16[1,2,2,2,128,128]{4,5,1,3,0,2:T(8,128)(2,1)S(1)}, u32[]{:S(2)}, u32[]{:S(2)}) collective-permute-start(bf16[1,2,2,2,128,128]{4,5,1,3,0,2:T(8,128)(2,1)S(1)} %collective-permute-done.32), channel_id=1, source_target_pairs={{0,1},{1,2},{2,3},{3,4},{4,5},{5,6},{6,7},{7,8},{8,9},{9,10},{10,1... | collective-permute-start | bytes 786440 | tf_op jit(solution)/shard_map/ppermute | solution.py:18
  536.4 26.8 %collective-permute-start.23 = (bf16[2,6,2,2,128,128]{4,5,1,3,2,0:T(8,128)(2,1)S(1)}, bf16[2,6,2,2,128,128]{4,5,1,3,2,0:T(8,128)(2,1)S(1)}, u32[]{:S(2)}, u32[]{:S(2)}) collective-permute-start(bf16[2,6,2,2,128,128]{4,5,1,3,2,0:T(8,128)(2,1)S(1)} %pad_maximum_fusion.9), channel_id=1, source_target_pairs={{0,32},{32,0},{64,96},{96,64},{1,33},{33,1},{65,97},{97,65},{2,34}... | collective-permute-start | bytes 4718600 | tf_op jit(solution)/shard_map/ppermute | solution.py:226
  538.9 14.1 %collective-permute-start.34 = (bf16[1,2,2,2,128,128]{4,5,1,3,0,2:T(8,128)(2,1)S(1)}, bf16[1,2,2,2,128,128]{4,5,1,3,0,2:T(8,128)(2,1)S(1)}, u32[]{:S(2)}, u32[]{:S(2)}) collective-permute-start(bf16[1,2,2,2,128,128]{4,5,1,3,0,2:T(8,128)(2,1)S(1)} %collective-permute-done.32), channel_id=1, source_target_pairs={{1,0},{2,1},{3,2},{4,3},{5,4},{6,5},{7,6},{8,7},{9,8},{10,9},{11,1... | collective-permute-start | bytes 786440 | tf_op jit(solution)/shard_map/ppermute | solution.py:21
  544.5 13.7 %collective-permute-start.31 = (bf16[1,2,2,2,128,128]{4,5,1,3,0,2:T(8,128)(2,1)S(1)}, bf16[1,2,2,2,128,128]{4,5,1,3,0,2:T(8,128)(2,1)S(1)}, u32[]{:S(2)}, u32[]{:S(2)}) collective-permute-start(bf16[1,2,2,2,128,128]{4,5,1,3,0,2:T(8,128)(2,1)S(1)} %pad_maximum_fusion.19), channel_id=1, source_target_pairs={{1,0},{2,1},{3,2},{4,3},{5,4},{6,5},{7,6},{8,7},{9,8},{10,9},{11,1... | collective-permute-start | bytes 786440 | tf_op jit(solution)/shard_map/ppermute | solution.py:21
  558.4 7.3 %collective-permute-start.35 = (bf16[2,6,2,2,128,128]{4,5,1,3,0,2:T(8,128)(2,1)S(1)}, bf16[2,6,2,2,128,128]{4,5,1,3,0,2:T(8,128)(2,1)S(1)}, u32[]{:S(2)}, u32[]{:S(2)}) collective-permute-start(bf16[2,6,2,2,128,128]{4,5,1,3,0,2:T(8,128)(2,1)S(1)} %pad_maximum_fusion.11), channel_id=1, source_target_pairs={{0,32},{32,0},{64,96},{96,64},{1,33},{33,1},{65,97},{97,65},{2,34}... | collective-permute-start | bytes 4718600 | tf_op jit(solution)/shard_map/ppermute | solution.py:226
  (72 other events, 397.4 us)
